TPU v7x, 128 devices: a whole 4x4x4 slice. The times are simulated.
128 devices in a mesh: gx: 8 (over z_hi, x), gy: 16 (over z_lo, y, core).
Axes of the slice: x: 4, y: 4, z: 4 (z_hi: 2, z_lo: 2; z = z_hi * 2 + z_lo), core: 2. Of those that a mesh axis runs over, the one named last changes fastest.
Arguments:
- populations: float32 [19, 128, 512, 256], P(None, 'gx', 'gy'), may hold values from 0.02 to 0.08
- ions: float32 [2, 128, 512, 256], P(None, 'gx', 'gy'), may hold values from 0.4 to 1.62, as said below
- mask: int32 [128, 512, 256], P('gx', 'gy'), may hold values from 0 to 1, as said below
Outputs:
- populations_out: float32 [19, 128, 512, 256], P(None, 'gx', 'gy')
- ions_out: float32 [2, 128, 512, 256], P(None, 'gx', 'gy')
- potential: float32 [128, 512, 256], P('gx', 'gy')
Inputs may be any that keep to these rules, and one draw needn't show every extreme that they name: `mask`: 1 marks a solid cell: every cell with second index 0 or 511 or third index 0 or 255, and scattered cells elsewhere; 0 marks fluid. `ions`: positive concentrations.
All inputs are finite; a program needn't handle non-finite values.
Results may differ from a plain program's by a relative error of at most 0.0004.
Values sent between devices are 32-bit elements; how exact they have to be, the bound alone decides.
No kernel may reach another device: no remote copies, remote signals or barrier semaphores. Data moves between devices by JAX's collectives and lax.ppermute only.
A program may use at most 128 MiB of HBM per device.

v0:
```python
import math

import jax
import jax.numpy as jnp
from jax import lax
from jax.experimental import pallas as pl
from jax.experimental.pallas import tpu as pltpu
from jax.sharding import PartitionSpec as P

PRECISE = lax.Precision.HIGHEST
SOLVE = lax.Precision.HIGH
LATTICE_VELOCITY = [
    (0, 0, 0),
    (1, 0, 0),
    (-1, 0, 0),
    (0, 1, 0),
    (0, -1, 0),
    (0, 0, 1),
    (0, 0, -1),
    (1, 1, 0),
    (-1, -1, 0),
    (1, -1, 0),
    (-1, 1, 0),
    (1, 0, 1),
    (-1, 0, -1),
    (1, 0, -1),
    (-1, 0, 1),
    (0, 1, 1),
    (0, -1, -1),
    (0, 1, -1),
    (0, -1, 1),
]
WEIGHTS = [1.0 / 3.0] + [1.0 / 18.0] * 6 + [1.0 / 36.0] * 12
OPPOSITE = [0, 2, 1, 4, 3, 6, 5, 8, 7, 10, 9, 12, 11, 14, 13, 16, 15, 18, 17]
RELAXATION = 0.8
SCREENING = 0.001
WALL_CHARGE = -0.1
FIELD_EXT = 0.3
DIFFUSIVITY = 0.1

PLUS_X = [i for i in range(19) if LATTICE_VELOCITY[i][0] == 1]
MINUS_X = [i for i in range(19) if LATTICE_VELOCITY[i][0] == -1]
PLUS_Y = [i for i in range(19) if LATTICE_VELOCITY[i][1] == 1]
MINUS_Y = [i for i in range(19) if LATTICE_VELOCITY[i][1] == -1]
CROSS_X = PLUS_X + MINUS_X
CROSS_Y = PLUS_Y + MINUS_Y
DIAGONAL = [7, 8, 9, 10]


def ring(axis, step):
    count = lax.axis_size(axis)
    return [(i, (i + step) % count) for i in range(count)]


def halos(block, axis, dim):
    n = block.shape[dim]
    low = lax.ppermute(lax.slice_in_dim(block, n - 1, n, axis=dim), axis, ring(axis, 1))
    high = lax.ppermute(lax.slice_in_dim(block, 0, 1, axis=dim), axis, ring(axis, -1))
    return low, high


def diagonal_pairs(step_x, step_y):
    nx = lax.axis_size("gx")
    ny = lax.axis_size("gy")
    pairs = []
    for a in range(nx):
        for b in range(ny):
            pairs.append((a * ny + b, ((a + step_x) % nx) * ny + (b + step_y) % ny))
    return pairs


def sine_table(length):
    series = jnp.arange(length, dtype=jnp.int32) + 1
    product = series[:, None] * series[None, :] % (2 * (length + 1))
    return jnp.sin(product.astype(jnp.float32) * (math.pi / (length + 1)))


def fourier_pair(length):
    series = jnp.arange(length, dtype=jnp.int32)
    product = series[:, None] * series[None, :] % length
    angles = product.astype(jnp.float32) * (2.0 * math.pi / length)
    return jnp.stack([jnp.cos(angles), -jnp.sin(angles)])


def wall_eigen(first, number, total):
    modes = (jnp.arange(number, dtype=jnp.int32) + first + 1).astype(jnp.float32)
    return 2.0 - 2.0 * jnp.cos(modes * (math.pi / (total + 1)))


def cycle_angles(first, number, total):
    modes = jnp.arange(number, dtype=jnp.int32) + first
    return modes.astype(jnp.float32) * (2.0 * math.pi / total)


def solve_potential(charge):
    len_local, wid_local, depth = charge.shape
    len_parts = lax.axis_size("gx")
    wid_parts = lax.axis_size("gy")
    devices = len_parts * wid_parts
    modes_local = depth // devices
    full_len = len_local * len_parts
    full_wid = wid_local * wid_parts
    me = lax.axis_index("gx") * wid_parts + lax.axis_index("gy")
    depth_sine, wid_sine, pair_full = lax.optimization_barrier(
        (sine_table(depth), sine_table(full_wid), fourier_pair(full_len))
    )
    flat = charge.reshape(len_local * wid_local, depth)
    sectioned = jnp.einsum("pz,nz->np", flat, depth_sine, precision=SOLVE)
    chunk = modes_local * len_local * wid_local
    sectioned = sectioned.reshape(devices, chunk // 128, 128)
    plane = lax.all_to_all(sectioned, ("gx", "gy"), 0, 0, tiled=True)
    plane = plane.reshape(len_parts, wid_parts, modes_local, len_local, wid_local)
    pair = pair_full.reshape(2, full_len, len_parts, len_local)
    spectra = jnp.einsum("rkax,abnxy->rknby", pair, plane, precision=SOLVE)
    spectra = spectra.reshape(2, full_len, modes_local, full_wid)
    spectra = jnp.einsum("my,rkny->rknm", wid_sine, spectra, precision=SOLVE)
    angles = cycle_angles(0, full_len, full_len)
    denom = (
        SCREENING
        + (2.0 - 2.0 * jnp.cos(angles))[:, None, None]
        + wall_eigen(me * modes_local, modes_local, depth)[None, :, None]
        + wall_eigen(0, full_wid, full_wid)[None, None, :]
    )
    spectra = spectra / denom[None]
    level = jnp.einsum("ym,rknm->rkny", wid_sine, spectra, precision=SOLVE) * (
        2.0 / (full_wid + 1)
    )
    plane = jnp.einsum("rkX,rknY->nXY", pair_full, level, precision=SOLVE) * (
        1.0 / full_len
    )
    plane = jnp.concatenate([plane[:, -1:], plane, plane[:, :1]], axis=1)
    plane = jnp.pad(plane, ((0, 0), (0, 0), (1, 1)))
    blocks = jnp.stack(
        [
            plane[:, a * len_local : a * len_local + len_local + 2, b * wid_local : b * wid_local + wid_local + 2]
            for a in range(len_parts)
            for b in range(wid_parts)
        ]
    )
    back = lax.all_to_all(blocks, ("gx", "gy"), 0, 0, tiled=True)
    back = back.reshape(depth, len_local + 2, wid_local + 2)
    return jnp.einsum("nz,nxy->xyz", depth_sine, back, precision=SOLVE) * (2.0 / (depth + 1))


def signed_sum(terms):
    total = None
    for sign, value in terms:
        if total is None:
            total = value if sign > 0 else -value
        else:
            total = total + value if sign > 0 else total - value
    return total


def collide(populations, distribution_tuple, volumetric_push):
    density = populations[0]
    for entry in range(1, 19):
        density = density + populations[entry]
    inverse = 1.0 / density
    velocity = []
    for component in range(3):
        moment = signed_sum(
            [(LATTICE_VELOCITY[e][component], populations[e]) for e in range(19) if LATTICE_VELOCITY[e][component] != 0]
        )
        velocity.append((moment + 0.5 * volumetric_push[component]) * inverse)
    speed_sq = velocity[0] * velocity[0] + velocity[1] * velocity[1] + velocity[2] * velocity[2]
    power = (
        velocity[0] * volumetric_push[0]
        + velocity[1] * volumetric_push[1]
        + velocity[2] * volumetric_push[2]
    )
    base = density * (1.0 - 1.5 * speed_sq)
    power3 = 3.0 * power
    keep = 1.0 - 1.0 / RELAXATION
    fluid = distribution_tuple > 0.5
    posts = []
    for entry in range(19):
        along = LATTICE_VELOCITY[entry]
        weight = WEIGHTS[entry]
        if entry == 0:
            equil = base
            source = -power3
        else:
            proj_vel = signed_sum([(along[c], velocity[c]) for c in range(3) if along[c] != 0])
            proj_force = signed_sum([(along[c], volumetric_push[c]) for c in range(3) if along[c] != 0])
            equil = base + density * proj_vel * (3.0 + 4.5 * proj_vel)
            source = proj_force * (3.0 + 9.0 * proj_vel) - power3
        moved = (
            keep * populations[entry]
            + (weight / RELAXATION) * equil
            + ((1.0 - 0.5 / RELAXATION) * weight) * source
        )
        posts.append(jnp.where(fluid, moved, populations[OPPOSITE[entry]]))
    return (posts, velocity)


def stream_kernel(pop_ref, fluid_ref, push_ref, out_ref, vel_ref, cols_ref):
    rows = pop_ref.shape[1]
    len_local, wid_local, depth = out_ref.shape[1:]

    def one_row(row, carry):
        pops = [pop_ref[entry, row] for entry in range(19)]
        push = [push_ref[component, row] for component in range(3)]
        posts, velocity = collide(pops, fluid_ref[row], push)
        here = pl.program_id(0) * rows + row
        for entry in range(19):
            cx, cy, cz = LATTICE_VELOCITY[entry]
            moved = posts[entry]
            if cy != 0:
                moved = pltpu.roll(moved, cy % wid_local, 0)
            if cz != 0:
                moved = pltpu.roll(moved, cz % depth, 1)
            target = (here + cx + len_local) % len_local
            out_ref[entry, target] = moved
            if cy != 0:
                at = 0 if cy == 1 else wid_local - 1
                cols_ref[CROSS_Y.index(entry), target] = moved[at : at + 1]
        for component in range(3):
            vel_ref[component, row] = velocity[component]
        return carry

    lax.fori_loop(0, rows, one_row, 0)


def stream_call(populations, distribution_tuple, push):
    entries, len_local, wid_local, depth = populations.shape
    rows = 2
    big = lambda n: pl.BlockSpec((n, rows, wid_local, depth), lambda i: (0, i, 0, 0))
    return pl.pallas_call(
        stream_kernel,
        grid=(len_local // rows,),
        in_specs=[big(entries), pl.BlockSpec((rows, wid_local, depth), lambda i: (i, 0, 0)), big(3)],
        out_specs=[
            pl.BlockSpec(populations.shape, lambda i: (0, 0, 0, 0)),
            big(3),
            pl.BlockSpec((len(CROSS_Y), len_local, 1, depth), lambda i: (0, 0, 0, 0)),
        ],
        out_shape=[
            jax.ShapeDtypeStruct(populations.shape, jnp.float32),
            jax.ShapeDtypeStruct((3, len_local, wid_local, depth), jnp.float32),
            jax.ShapeDtypeStruct((len(CROSS_Y), len_local, 1, depth), jnp.float32),
        ],
        compiler_params=pltpu.CompilerParams(vmem_limit_bytes=48 * 1024 * 1024),
    )(populations, distribution_tuple, push)


def patch_kernel(rows_ref, cols_ref, wrapped_hbm, out_hbm, sems):
    del wrapped_hbm
    len_local, wid_local = out_hbm.shape[1:3]
    first = []
    for k, entry in enumerate(CROSS_X):
        at = 0 if LATTICE_VELOCITY[entry][0] == 1 else len_local - 1
        first.append(pltpu.make_async_copy(rows_ref.at[k], out_hbm.at[entry, pl.ds(at, 1)], sems.at[k]))
    for copy in first:
        copy.start()
    for copy in first:
        copy.wait()
    second = []
    for k, entry in enumerate(CROSS_Y):
        at = 0 if LATTICE_VELOCITY[entry][1] == 1 else wid_local - 1
        second.append(
            pltpu.make_async_copy(
                cols_ref.at[k], out_hbm.at[entry, :, pl.ds(at, 1)], sems.at[len(first) + k]
            )
        )
    for copy in second:
        copy.start()
    for copy in second:
        copy.wait()


def patch_call(rows, cols, wrapped):
    vmem = pl.BlockSpec(memory_space=pltpu.VMEM)
    return pl.pallas_call(
        patch_kernel,
        in_specs=[vmem, vmem, pl.BlockSpec(memory_space=pl.ANY)],
        out_specs=pl.BlockSpec(memory_space=pl.ANY),
        out_shape=jax.ShapeDtypeStruct(wrapped.shape, wrapped.dtype),
        scratch_shapes=[pltpu.SemaphoreType.DMA((len(CROSS_X) + len(CROSS_Y),))],
        input_output_aliases={2: 0},
    )(rows, cols, wrapped)


def drift_diffuse(
    conc,
    neighbour_cells,
    distribution_tuple,
    velocity,
    gradient_of_voltage,
    potential,
    free_electrostatic_share,
):
    laplace = -6.0 * conc
    drift = conc * (SCREENING * potential - free_electrostatic_share)[None]
    advect = jnp.zeros_like(conc)
    for component in range(3):
        upper, lower = neighbour_cells[component]
        up_val = upper[2:3] * upper[:2] + (1.0 - upper[2:3]) * conc
        low_val = lower[2:3] * lower[:2] + (1.0 - lower[2:3]) * conc
        laplace = laplace + up_val + low_val
        slope = 0.5 * (up_val - low_val)
        drift = drift - slope * gradient_of_voltage[component][None]
        advect = advect + slope * velocity[component][None]
    valence = jnp.asarray([1.0, -1.0], jnp.float32)[:, None, None, None]
    change = DIFFUSIVITY * (laplace + valence * drift) - advect
    return conc + distribution_tuple[None] * change


def shift_x(block, low, high, step, dim):
    if step == 1:
        return jnp.concatenate([low, lax.slice_in_dim(block, 0, block.shape[dim] - 1, axis=dim)], dim)
    if step == -1:
        return jnp.concatenate([lax.slice_in_dim(block, 1, None, axis=dim), high], dim)
    return block


def body(populations, ions, mask):
    len_local, wid_local, depth = mask.shape
    wid_parts = lax.axis_size("gy")
    wid_index = lax.axis_index("gy")
    distribution_tuple = (mask == 0).astype(jnp.float32)
    ionic = jnp.concatenate([ions, distribution_tuple[None]], axis=0)
    ionic_x = halos(ionic, "gx", 1)
    ionic_y = halos(ionic, "gy", 2)
    free_electrostatic_share = (
        distribution_tuple * (ions[0] - ions[1]) + (1.0 - distribution_tuple) * WALL_CHARGE
    )
    extended = solve_potential(free_electrostatic_share)
    potential = extended[1:-1, 1:-1]
    field_len = FIELD_EXT - 0.5 * (extended[2:, 1:-1] - extended[:-2, 1:-1])
    field_wid = -0.5 * (extended[1:-1, 2:] - extended[1:-1, :-2])
    depth_pad = jnp.pad(potential, ((0, 0), (0, 0), (1, 1)))
    field_depth = -0.5 * (depth_pad[:, :, 2:] - depth_pad[:, :, :-2])
    gradient_of_voltage = [field_len, field_wid, field_depth]
    ion_concentration_sum = distribution_tuple * free_electrostatic_share
    volumetric_push = [ion_concentration_sum * voltage_grid for voltage_grid in gradient_of_voltage]
    push = jnp.stack(volumetric_push)
    wrapped, velocity, edge_cols = stream_call(populations, distribution_tuple, push)
    velocity = [velocity[component] for component in range(3)]
    last_x = len_local - 1
    last_y = wid_local - 1
    edge_x = {1: 0, -1: last_x}
    edge_y = {1: 0, -1: last_y}
    rows = {}
    cols = {}
    for step in (1, -1):
        group = [e for e in range(19) if LATTICE_VELOCITY[e][0] == step]
        sent = jnp.stack([wrapped[e, edge_x[step]] for e in group])
        got = lax.ppermute(sent, "gx", ring("gx", step))
        rows.update({e: got[k] for k, e in enumerate(group)})
    for step in (1, -1):
        group = [e for e in range(19) if LATTICE_VELOCITY[e][1] == step]
        pieces = []
        for e in group:
            column = edge_cols[CROSS_Y.index(e)]
            cx = LATTICE_VELOCITY[e][0]
            if cx != 0:
                cell = rows[e][edge_y[step]][None, None]
                if edge_x[cx] == 0:
                    column = jnp.concatenate([cell, column[1:]])
                else:
                    column = jnp.concatenate([column[:-1], cell])
            pieces.append(column)
        got = lax.ppermute(jnp.stack(pieces), "gy", ring("gy", step))
        cols.update({e: got[k] for k, e in enumerate(group)})
    populations_out = patch_call(
        jnp.stack([rows[e][None] for e in CROSS_X]),
        jnp.stack([cols[e] for e in CROSS_Y]),
        wrapped,
    )

    low_ix, high_ix = ionic_x
    low_iy, high_iy = ionic_y
    neighbour_cells = [
        (shift_x(ionic, None, high_ix, -1, 1), shift_x(ionic, low_ix, None, 1, 1)),
        (shift_x(ionic, None, high_iy, -1, 2), shift_x(ionic, low_iy, None, 1, 2)),
        (jnp.roll(ionic, -1, 3), jnp.roll(ionic, 1, 3)),
    ]
    ions_out = drift_diffuse(
        ions,
        neighbour_cells,
        distribution_tuple,
        velocity,
        gradient_of_voltage,
        potential,
        free_electrostatic_share,
    )
    return (populations_out, ions_out, potential)


def solution(mesh):
    placed = (P(None, "gx", "gy", None), P(None, "gx", "gy", None), P("gx", "gy", None))
    return jax.shard_map(
        body,
        mesh=mesh,
        in_specs=placed,
        out_specs=(P(None, "gx", "gy", None), P(None, "gx", "gy", None), P("gx", "gy", None)),
        check_vma=False,
    )
```

profile of v0, /device:TPU:0, one launch (start us, length us, event | category | flops | bytes accessed | tf_op | source)
XLA Modules:
  0.0 142.4 jit_solution(2399607086213663911)
XLA Ops:
  3.2 5.0 %fusion.14 = f32[512,512]{1,0:T(8,128)} fusion(s32[512]{0:T(512)S(1)} %iota_add_fusion), kind=kLoop, calls=%fused_computation.40 | loop fusion | flops 2359296 | bytes 1050624 | tf_op jit(solution)/shard_map/sin | solution.py:75
  10.3 11.7 %all-to-all-start = ((f32[128,8,128]{2,1,0:T(8,128)}), f32[128,8,128]{2,1,0:T(8,128)}, u32[]{:S(2)}, u32[]{:S(2)}) async-start(f32[128,8,128]{2,1,0:T(8,128)} %reshape.198), calls=%async_computation | async-start | bytes 1048576 | tf_op jit(solution)/shard_map/all_to_all | solution.py:111
  22.7 3.9 %collective-permute-start.6 = (f32[3,16,1,256]{3,2,1,0:T(1,128)}, f32[3,16,1,256]{3,2,1,0:T(1,128)}, u32[]{:S(2)}, u32[]{:S(2)}) collective-permute-start(f32[3,16,1,256]{3,2,1,0:T(1,128)} %get-tuple-element.50), channel_id=1, source_target_pairs={{0,15},{1,0},{2,1},{3,2},{4,3},{5,4},{6,5},{7,6},{8,7},{9,8},{10,9... | collective-permute-start | bytes 147464 | tf_op jit(solution)/shard_map/ppermute | solution.py:58
  28.2 4.8 %collective-permute-start.4 = (f32[3,1,32,256]{3,2,1,0:T(8,128)}, f32[3,1,32,256]{3,2,1,0:T(8,128)}, u32[]{:S(2)}, u32[]{:S(2)}) collective-permute-start(f32[3,1,32,256]{3,2,1,0:T(8,128)} %get-tuple-element.46), channel_id=1, source_target_pairs={{0,112},{16,0},{32,16},{48,32},{64,48},{80,64},{96,80},{112,96},{1... | collective-permute-start | bytes 294920 | tf_op jit(solution)/shard_map/ppermute | solution.py:58
  35.0 2.1 %fusion.2 = (f32[3,16,31,256]{3,2,1,0:T(8,128)}, f32[3,16,31,256]{3,2,1,0:T(8,128)}) fusion(f32[2,16,32,256]{3,2,1,0:T(8,128)S(1)} %copy-done, f32[1,16,32,256]{3,2,1,0:T(8,128)S(1)} %get-tuple-element.25), kind=kLoop, calls=%fused_computation.24 | loop fusion | flops 761856 | bytes 4620288 | tf_op jit(solution)/shard_map/concatenate | solution.py:322
  37.1 2.0 %fusion.5 = (f32[3,15,32,256]{3,2,1,0:T(8,128)}, f32[3,15,32,256]{3,2,1,0:T(8,128)}) fusion(f32[2,16,32,256]{3,2,1,0:T(8,128)S(1)} %copy-done, f32[1,16,32,256]{3,2,1,0:T(8,128)S(1)} %get-tuple-element.25), kind=kLoop, calls=%fused_computation.29 | loop fusion | flops 737280 | bytes 4521984 | tf_op jit(solution)/shard_map/concatenate | solution.py:322
  40.2 2.7 %reshape.199 = f32[8,16,2,16,32]{4,3,2,1,0:T(8,128)} reshape(f32[128,8,128]{2,1,0:T(8,128)} %all-to-all-done) | data formatting | bytes 1048576 | tf_op jit(solution)/shard_map/reshape | solution.py:112
  42.9 3.5 %fusion.7 = f32[2,128,2,16,32]{1,4,0,2,3:T(8,128)S(1)} fusion(f32[2,128,8,16,1,1]{1,3,2,0,5,4:T(8,128)} %bitcast.683, f32[8,16,2,16,32]{4,3,2,1,0:T(8,128)} %reshape.199), kind=kOutput, calls=%fused_computation.31 | convolution fusion | flops 201326592 | bytes 1703936 | tf_op jit(solution)/shard_map/rkax,abnxy->rknby/dot_general | solution.py:114
  59.7 2.6 %copy.304 = f32[128,2,18,34]{3,1,2,0:T(2,128)} copy(f32[128,2,18,34]{3,2,1,0:T(8,128)S(1)} %constant_dynamic-update-slice_fusion) | data formatting | bytes 1253376 | tf_op jit(solution)/shard_map/stack | solution.py:133
  62.3 5.3 %reshape.210 = f32[128,1,1224]{2,1,0:T(1,128)} reshape(f32[128,18,2,34]{3,2,1,0:T(2,128)} %bitcast.677) | data formatting | bytes 1253376
  67.5 5.9 %all-to-all-start.1 = ((f32[128,1,1224]{2,1,0:T(1,128)}), f32[128,1,1224]{2,1,0:T(1,128)}, u32[]{:S(2)}, u32[]{:S(2)}) async-start(f32[128,1,1224]{2,1,0:T(1,128)} %reshape.210), calls=%async_computation.1 | async-start | bytes 1310720 | tf_op jit(solution)/shard_map/all_to_all | solution.py:140
  73.5 2.9 %subtract_bitcast_fusion = (f32[16,32,256]{2,1,0:T(8,128)}, f32[1,16,32,256]{3,2,1,0:T(8,128)}, f32[16,32,256]{2,1,0:T(8,128)}, f32[1,16,32,256]{3,2,1,0:T(8,128)}) fusion(f32[1,16,32,256]{3,2,1,0:T(8,128)S(1)} %get-tuple-element.25, f32[2,16,32,256]{3,2,1,0:T(8,128)S(1)} %copy-done, f32[3,16,32,1]{3,2,1,0:T(8,128)} %get-tuple-element.53, ...), kind=kLoop, calls=%fused_computation.94 | loop fusion | flops 655360 | bytes 5249024 | tf_op jit(solution)/shard_map/mul | solution.py:299
  76.4 2.0 %subtract_bitcast_fusion.2 = (f32[16,32,256]{2,1,0:T(8,128)}, f32[1,16,32,256]{3,2,1,0:T(8,128)}) fusion(f32[3,16,31,256]{3,2,1,0:T(8,128)S(1)} %copy-done.3, f32[3,16,1,256]{3,2,1,0:T(1,128)} %collective-permute-done.7), kind=kLoop, calls=%fused_computation.96 | loop fusion | flops 262144 | bytes 2621440 | tf_op jit(solution)/shard_map/mul | solution.py:299
  78.4 1.9 %subtract_bitcast_fusion.3 = (f32[16,32,256]{2,1,0:T(8,128)}, f32[1,16,32,256]{3,2,1,0:T(8,128)}) fusion(f32[3,16,1,256]{3,2,1,0:T(1,128)} %collective-permute-done.6, f32[3,16,31,256]{3,2,1,0:T(8,128)S(1)} %copy-done.1), kind=kLoop, calls=%fused_computation.97 | loop fusion | flops 262144 | bytes 2621440 | tf_op jit(solution)/shard_map/mul | solution.py:298
  84.1 3.7 %all-to-all-done.1 = f32[128,1,1224]{2,1,0:T(1,128)} async-done(((f32[128,1,1224]{2,1,0:T(1,128)}), f32[128,1,1224]{2,1,0:T(1,128)}, u32[]{:S(2)}, u32[]{:S(2)}) %all-to-all-start.1) | async-done | bytes 626720 | tf_op jit(solution)/shard_map/all_to_all | solution.py:140
  88.3 3.3 %reduce = f32[128,1224]{1,0:T(8,128)S(1)} reduce(f32[128,1,1224]{2,1,0:T(1,128)} %all-to-all-done.1, f32[]{:T(128)} %broadcast.284), dimensions={1}, to_apply=%all_to_all.7.reduce_sub_computation | reduce | bytes 1253380 | tf_op jit(solution)/shard_map/all_to_all | solution.py:140
  91.6 3.6 %reshape.211 = f32[128,18,2,34]{3,2,1,0:T(2,128)} reshape(f32[128,1224]{1,0:T(8,128)S(1)} %reduce) | data formatting | bytes 1253376
  95.3 3.0 %copy.286 = f32[128,2,18,34]{3,1,0,2:T(2,128)S(1)} copy(f32[128,2,18,34]{3,1,2,0:T(2,128)} %bitcast.676) | data formatting | bytes 1253376 | tf_op jit(solution)/shard_map/all_to_all | solution.py:140
  98.3 2.0 %convolution_multiply_fusion.1 = f32[18,34,256]{2,1,0:T(8,128)S(1)} fusion(f32[256,18,34]{2,0,1:T(8,128)S(1)} %bitcast.675, f32[256,256]{1,0:T(8,128)S(1)} %fusion.42), kind=kOutput, calls=%fused_computation.34 | convolution fusion | flops 240804864 | bytes 1515520 | tf_op jit(solution)/shard_map/nz,nxy->xyz/dot_general | solution.py:142
  101.8 15.4 %shard_map.67 = (f32[19,16,32,256]{3,2,1,0:T(8,128)}, f32[3,16,32,256]{3,2,1,0:T(8,128)S(1)}, f32[10,16,1,256]{3,2,1,0:T(1,128)S(1)}) custom-call(f32[19,16,32,256]{3,2,1,0:T(8,128)} %pop_ref.1, f32[16,32,256]{2,1,0:T(8,128)S(1)} %convert_element_type.50.fluid_ref, f32[3,16,32,256]{3,2,1,0:T(8,128)S(1)} %pad_maximum_fusion.push_ref), custom_call_target="tpu_custom_call" | custom-call | tf_op jit(solution)/shard_map/pallas_call | solution.py:229
  122.1 5.1 %collective-permute-start.1 = (f32[5,32,256]{2,1,0:T(8,128)S(1)}, f32[5,32,256]{2,1,0:T(8,128)S(1)}, u32[]{:S(2)}, u32[]{:S(2)}) collective-permute-start(f32[5,32,256]{2,1,0:T(8,128)S(1)} %get-tuple-element.27), channel_id=1, source_target_pairs={{0,112},{16,0},{32,16},{48,32},{64,48},{80,64},{96,80},{112,96},{1... | collective-permute-start | bytes 491528 | tf_op jit(solution)/shard_map/ppermute | solution.py:349
  127.5 4.9 %multiply_add_fusion = f32[2,16,32,256]{3,2,1,0:T(8,128)} fusion(f32[2,16,32,256]{3,2,1,0:T(8,128)S(1)} %copy-done, f32[1,16,32,256]{3,2,1,0:T(8,128)S(1)} %get-tuple-element.25, f32[3,16,32,1]{3,2,1,0:T(8,128)S(1)} %copy-done.14, f32[3,16,32,1]{3,2,1,0:T(8,128)S(1)} %copy-done.13, f32[3,16,32,255]{3,2,1,0:T(8,128)S(1)} %copy-done.6, ...), kind=kLoop, calls=%fused_computation.63 | loop fusion | flops 13893632 | bytes 20977672 | tf_op jit(solution)/shard_map/add | solution.py:306
  134.7 4.1 %collective-permute-done.2 = f32[5,16,1,256]{3,2,1,0:T(1,128)S(1)} collective-permute-done((f32[5,16,1,256]{3,2,1,0:T(1,128)S(1)}, f32[5,16,1,256]{3,2,1,0:T(1,128)S(1)}, u32[]{:S(2)}, u32[]{:S(2)}) %collective-permute-start.2) | collective-permute-done | bytes 81952 | tf_op jit(solution)/shard_map/ppermute | solution.py:364
  139.7 2.6 %shard_map.68 = f32[19,16,32,256]{3,2,1,0:T(8,128)} custom-call(f32[10,1,32,256]{3,2,1,0:T(8,128)} %copy-done.24, f32[10,16,1,256]{3,2,1,0:T(1,128)} %pad_maximum_fusion.14.cols_ref, f32[19,16,32,256]{3,2,1,0:T(8,128)} %get-tuple-element.12.wrapped_hbm), custom_call_target="tpu_custom_call", output_to_operand_aliasing={{}: (2, {})} | custom-call | tf_op jit(solution)/shard_map/pallas_call | solution.py:274
  (252 shorter events, 36.9 us)
Async XLA Ops:
  9.0 18.3 %copy-start.11 = (f32[16,32,256]{2,1,0:T(8,128)}, f32[16,32,256]{2,1,0:T(8,128)S(1)}, u32[]{:S(2)}) copy-start(f32[16,32,256]{2,1,0:T(8,128)S(1)} %fusion.39) | copy-start | bytes 1572868
  10.3 29.9 %all-to-all-start = ((f32[128,8,128]{2,1,0:T(8,128)}), f32[128,8,128]{2,1,0:T(8,128)}, u32[]{:S(2)}, u32[]{:S(2)}) async-start(f32[128,8,128]{2,1,0:T(8,128)} %reshape.198), calls=%async_computation | async-start | bytes 1048576 | tf_op jit(solution)/shard_map/all_to_all | solution.py:111
  22.7 53.7 %collective-permute-start.7 = (f32[3,16,1,256]{3,2,1,0:T(1,128)}, f32[3,16,1,256]{3,2,1,0:T(1,128)}, u32[]{:S(2)}, u32[]{:S(2)}) collective-permute-start(f32[3,16,1,256]{3,2,1,0:T(1,128)} %get-tuple-element.51), channel_id=1, source_target_pairs={{0,1},{1,2},{2,3},{3,4},{4,5},{5,6},{6,7},{7,8},{8,9},{9,10},{10,1... | collective-permute-start | bytes 147464 | tf_op jit(solution)/shard_map/ppermute | solution.py:57
  22.7 55.6 %collective-permute-start.6 = (f32[3,16,1,256]{3,2,1,0:T(1,128)}, f32[3,16,1,256]{3,2,1,0:T(1,128)}, u32[]{:S(2)}, u32[]{:S(2)}) collective-permute-start(f32[3,16,1,256]{3,2,1,0:T(1,128)} %get-tuple-element.50), channel_id=1, source_target_pairs={{0,15},{1,0},{2,1},{3,2},{4,3},{5,4},{6,5},{7,6},{8,7},{9,8},{10,9... | collective-permute-start | bytes 147464 | tf_op jit(solution)/shard_map/ppermute | solution.py:58
  27.3 53.0 %collective-permute-start.5 = (f32[3,1,32,256]{3,2,1,0:T(8,128)}, f32[3,1,32,256]{3,2,1,0:T(8,128)}, u32[]{:S(2)}, u32[]{:S(2)}) collective-permute-start(f32[3,1,32,256]{3,2,1,0:T(8,128)} %get-tuple-element.47), channel_id=1, source_target_pairs={{0,16},{16,32},{32,48},{48,64},{64,80},{80,96},{96,112},{112,0},{1... | collective-permute-start | bytes 294920 | tf_op jit(solution)/shard_map/ppermute | solution.py:57
  28.2 54.0 %collective-permute-start.4 = (f32[3,1,32,256]{3,2,1,0:T(8,128)}, f32[3,1,32,256]{3,2,1,0:T(8,128)}, u32[]{:S(2)}, u32[]{:S(2)}) collective-permute-start(f32[3,1,32,256]{3,2,1,0:T(8,128)} %get-tuple-element.46), channel_id=1, source_target_pairs={{0,112},{16,0},{32,16},{48,32},{64,48},{80,64},{96,80},{112,96},{1... | collective-permute-start | bytes 294920 | tf_op jit(solution)/shard_map/ppermute | solution.py:58
  35.0 38.5 %copy-start.5 = (f32[3,16,32,255]{3,2,1,0:T(8,128)}, f32[3,16,32,255]{3,2,1,0:T(8,128)S(1)}, u32[]{:S(2)}) copy-start(f32[3,16,32,255]{3,2,1,0:T(8,128)S(1)} %fusion.4) | copy-start | bytes 4700164
  67.5 20.3 %all-to-all-start.1 = ((f32[128,1,1224]{2,1,0:T(1,128)}), f32[128,1,1224]{2,1,0:T(1,128)}, u32[]{:S(2)}, u32[]{:S(2)}) async-start(f32[128,1,1224]{2,1,0:T(1,128)} %reshape.210), calls=%async_computation.1 | async-start | bytes 1310720 | tf_op jit(solution)/shard_map/all_to_all | solution.py:140
  101.7 25.6 %copy-start.6 = (f32[3,16,32,255]{3,2,1,0:T(8,128)S(1)}, f32[3,16,32,255]{3,2,1,0:T(8,128)}, u32[]{:S(2)}) copy-start(f32[3,16,32,255]{3,2,1,0:T(8,128)} %copy-done.5) | copy-start | bytes 4700164
  101.7 25.6 %copy-start.8 = (f32[3,15,32,256]{3,2,1,0:T(8,128)S(1)}, f32[3,15,32,256]{3,2,1,0:T(8,128)}, u32[]{:S(2)}) copy-start(f32[3,15,32,256]{3,2,1,0:T(8,128)} %get-tuple-element.44) | copy-start | bytes 4423684
  101.7 25.6 %copy-start.10 = (f32[3,15,32,256]{3,2,1,0:T(8,128)S(1)}, f32[3,15,32,256]{3,2,1,0:T(8,128)}, u32[]{:S(2)}) copy-start(f32[3,15,32,256]{3,2,1,0:T(8,128)} %get-tuple-element.45) | copy-start | bytes 4423684
  101.7 25.6 %copy-start.14 = (f32[3,16,32,1]{3,2,1,0:T(8,128)S(1)}, f32[3,16,32,1]{3,2,1,0:T(8,128)}, u32[]{:S(2)}) copy-start(f32[3,16,32,1]{3,2,1,0:T(8,128)} %get-tuple-element.53) | copy-start | bytes 18436
  101.7 25.6 %copy-start.17 = (f32[16,32,256]{2,1,0:T(8,128)S(1)}, f32[16,32,256]{2,1,0:T(8,128)}, u32[]{:S(2)}) copy-start(f32[16,32,256]{2,1,0:T(8,128)} %get-tuple-element.39) | copy-start | bytes 1572868
  101.7 25.6 %copy-start.18 = (f32[16,32,256]{2,1,0:T(8,128)S(1)}, f32[16,32,256]{2,1,0:T(8,128)}, u32[]{:S(2)}) copy-start(f32[16,32,256]{2,1,0:T(8,128)} %get-tuple-element.40) | copy-start | bytes 1572868
  101.8 25.6 %copy-start.19 = (f32[16,32,256]{2,1,0:T(8,128)S(1)}, f32[16,32,256]{2,1,0:T(8,128)}, u32[]{:S(2)}) copy-start(f32[16,32,256]{2,1,0:T(8,128)} %get-tuple-element.37) | copy-start | bytes 1572868
  101.8 25.6 %copy-start.20 = (f32[16,32,256]{2,1,0:T(8,128)S(1)}, f32[16,32,256]{2,1,0:T(8,128)}, u32[]{:S(2)}) copy-start(f32[16,32,256]{2,1,0:T(8,128)} %get-tuple-element.38) | copy-start | bytes 1572868
  101.8 25.6 %copy-start.21 = (f32[16,32,256]{2,1,0:T(8,128)S(1)}, f32[16,32,256]{2,1,0:T(8,128)}, u32[]{:S(2)}) copy-start(f32[16,32,256]{2,1,0:T(8,128)} %get-tuple-element.17) | copy-start | bytes 1572868
  117.1 10.3 %copy-start.4 = (f32[3,16,31,256]{3,2,1,0:T(8,128)S(1)}, f32[3,16,31,256]{3,2,1,0:T(8,128)}, u32[]{:S(2)}) copy-start(f32[3,16,31,256]{3,2,1,0:T(8,128)} %get-tuple-element.49) | copy-start | bytes 4571140
  117.1 10.3 %copy-start.13 = (f32[3,16,32,1]{3,2,1,0:T(8,128)S(1)}, f32[3,16,32,1]{3,2,1,0:T(8,128)}, u32[]{:S(2)}) copy-start(f32[3,16,32,1]{3,2,1,0:T(8,128)} %get-tuple-element.52) | copy-start | bytes 18436
  117.1 10.3 %copy-start.25 = (f32[2]{0:T(128)S(1)}, f32[2]{0:T(128)}, u32[]{:S(2)}) copy-start(f32[2]{0:T(128)} %constant.105.clone) | copy-start | bytes 28
  121.5 10.9 %collective-permute-start = (f32[5,32,256]{2,1,0:T(8,128)S(1)}, f32[5,32,256]{2,1,0:T(8,128)S(1)}, u32[]{:S(2)}, u32[]{:S(2)}) collective-permute-start(f32[5,32,256]{2,1,0:T(8,128)S(1)} %get-tuple-element.28), channel_id=1, source_target_pairs={{0,16},{16,32},{32,48},{48,64},{64,80},{80,96},{96,112},{112,0},{1... | collective-permute-start | bytes 491528 | tf_op jit(solution)/shard_map/ppermute | solution.py:349
  122.1 10.4 %collective-permute-start.1 = (f32[5,32,256]{2,1,0:T(8,128)S(1)}, f32[5,32,256]{2,1,0:T(8,128)S(1)}, u32[]{:S(2)}, u32[]{:S(2)}) collective-permute-start(f32[5,32,256]{2,1,0:T(8,128)S(1)} %get-tuple-element.27), channel_id=1, source_target_pairs={{0,112},{16,0},{32,16},{48,32},{64,48},{80,64},{96,80},{112,96},{1... | collective-permute-start | bytes 491528 | tf_op jit(solution)/shard_map/ppermute | solution.py:349
  132.6 2.1 %collective-permute-start.3 = (f32[5,16,1,256]{3,2,1,0:T(1,128)S(1)}, f32[5,16,1,256]{3,2,1,0:T(1,128)S(1)}, u32[]{:S(2)}, u32[]{:S(2)}) collective-permute-start(f32[5,16,1,256]{3,2,1,0:T(1,128)S(1)} %pad_maximum_fusion.17), channel_id=1, source_target_pairs={{0,15},{1,0},{2,1},{3,2},{4,3},{5,4},{6,5},{7,6},{8,7},{9,8},{10,9... | collective-permute-start | bytes 245768 | tf_op jit(solution)/shard_map/ppermute | solution.py:364
  132.8 6.0 %collective-permute-start.2 = (f32[5,16,1,256]{3,2,1,0:T(1,128)S(1)}, f32[5,16,1,256]{3,2,1,0:T(1,128)S(1)}, u32[]{:S(2)}, u32[]{:S(2)}) collective-permute-start(f32[5,16,1,256]{3,2,1,0:T(1,128)S(1)} %pad_maximum_fusion.16), channel_id=1, source_target_pairs={{0,1},{1,2},{2,3},{3,4},{4,5},{5,6},{6,7},{7,8},{8,9},{9,10},{10,1... | collective-permute-start | bytes 245768 | tf_op jit(solution)/shard_map/ppermute | solution.py:364
  (12 other events, 53.6 us)
where the time goes:
time: 143 us; the launch traced here: 142 us
  other arithmetic  40.7 us (28%)
  starting transfers between devices  33.4 us (23%)
  local copies, waits for them, and re-layouts  30.4 us (21%)
  Pallas kernels  17.9 us (13%)
  matrix products  9.28 us (6%)
  waiting for transfers between devices  9.12 us (6%)
  between operations  1.55 us (1%)
    unnamed x166, local copies, waits for them, and re-layouts  19.8 us
    pallas_call x1, Pallas kernels, stream_call(): pl.pallas_call(stream_kernel, grid=(len_local // rows,), in_specs=[big(en...  15.4 us
    all_to_all x1, starting transfers between devices, solve_potential(): plane = lax.all_to_all(sectioned, ('gx', 'gy'), 0, 0, tiled=True)  11.7 us
    ppermute x2, starting transfers between devices, halos(): lax.ppermute(lax.slice_in_dim(block, 0, 1, axis=dim), axis, ring(axis, -1))  8.61 us
    concatenate x6, other arithmetic, body(): ionic = jnp.concatenate([ions, distribution_tuple[None]], axis=0)  7.52 us
    mul x3, other arithmetic, drift_diffuse(): low_val = lower[2:3] * lower[:2] + (1.0 - lower[2:3]) * conc  6.73 us
    sin x2, other arithmetic, sine_table(): return jnp.sin(product.astype(jnp.float32) * (math.pi / (length + 1)))  6.11 us
    all_to_all x1, starting transfers between devices, solve_potential(): back = lax.all_to_all(blocks, ('gx', 'gy'), 0, 0, tiled=True)  5.9 us
  transfers between devices with their start and end apart: 10, of which 3 were waited for; matrix products, arithmetic and copies ran while one was open for 36% of the time, Pallas kernels for 0%

commit v1 on v0

--- a/solution.py
+++ b/solution.py
@@ -101,9 +101,8 @@
     full_len = len_local * len_parts
     full_wid = wid_local * wid_parts
     me = lax.axis_index("gx") * wid_parts + lax.axis_index("gy")
-    depth_sine, wid_sine, pair_full = lax.optimization_barrier(
-        (sine_table(depth), sine_table(full_wid), fourier_pair(full_len))
-    )
+    depth_sine = lax.optimization_barrier(sine_table(depth))
+    wid_sine, pair_full = lax.optimization_barrier((sine_table(full_wid), fourier_pair(full_len)))
     flat = charge.reshape(len_local * wid_local, depth)
     sectioned = jnp.einsum("pz,nz->np", flat, depth_sine, precision=SOLVE)
     chunk = modes_local * len_local * wid_local

time: 143 us -> 144 us (level)
  transfers between devices with their start and end apart: 10 -> 10, of which waited for: 3 -> 3; matrix products, arithmetic and copies ran while one was open for 36% -> 40% of each run, Pallas kernels for 0% -> 0%
where the time goes in v1:
time: 144 us; the launch traced here: 143 us
  other arithmetic  42 us (29%)
  starting transfers between devices  33.2 us (23%)
  local copies, waits for them, and re-layouts  30.5 us (21%)
  Pallas kernels  17.9 us (12%)
  matrix products  9.28 us (6%)
  waiting for transfers between devices  9.12 us (6%)
  between operations  1.57 us (1%)
    unnamed x166, local copies, waits for them, and re-layouts  19.8 us
    pallas_call x1, Pallas kernels, stream_call(): pl.pallas_call(stream_kernel, grid=(len_local // rows,), in_specs=[big(en...  15.4 us
    all_to_all x1, starting transfers between devices, solve_potential(): plane = lax.all_to_all(sectioned, ('gx', 'gy'), 0, 0, tiled=True)  11.7 us
    ppermute x2, starting transfers between devices, halos(): lax.ppermute(lax.slice_in_dim(block, 0, 1, axis=dim), axis, ring(axis, -1))  8.61 us
    concatenate x6, other arithmetic, body(): ionic = jnp.concatenate([ions, distribution_tuple[None]], axis=0)  7.52 us
    mul x3, other arithmetic, drift_diffuse(): low_val = lower[2:3] * lower[:2] + (1.0 - lower[2:3]) * conc  6.73 us
    sin x2, other arithmetic, sine_table(): return jnp.sin(product.astype(jnp.float32) * (math.pi / (length + 1)))  6.08 us
    all_to_all x1, starting transfers between devices, solve_potential(): back = lax.all_to_all(blocks, ('gx', 'gy'), 0, 0, tiled=True)  5.68 us
  transfers between devices with their start and end apart: 10, of which 3 were waited for; matrix products, arithmetic and copies ran while one was open for 40% of the time, Pallas kernels for 0%

profile of v1, /device:TPU:0, one launch (start us, length us, event | category | flops | bytes accessed | tf_op | source)
XLA Modules:
  0.0 143.5 jit_solution(11433881318119632289)
XLA Ops:
  5.6 11.7 %all-to-all-start = ((f32[128,8,128]{2,1,0:T(8,128)}), f32[128,8,128]{2,1,0:T(8,128)}, u32[]{:S(2)}, u32[]{:S(2)}) async-start(f32[128,8,128]{2,1,0:T(8,128)} %reshape.198), calls=%async_computation | async-start | bytes 1048576 | tf_op jit(solution)/shard_map/all_to_all | solution.py:110
  18.0 3.9 %collective-permute-start.6 = (f32[3,16,1,256]{3,2,1,0:T(1,128)}, f32[3,16,1,256]{3,2,1,0:T(1,128)}, u32[]{:S(2)}, u32[]{:S(2)}) collective-permute-start(f32[3,16,1,256]{3,2,1,0:T(1,128)} %get-tuple-element.48), channel_id=1, source_target_pairs={{0,15},{1,0},{2,1},{3,2},{4,3},{5,4},{6,5},{7,6},{8,7},{9,8},{10,9... | collective-permute-start | bytes 147464 | tf_op jit(solution)/shard_map/ppermute | solution.py:58
  23.5 4.8 %collective-permute-start.4 = (f32[3,1,32,256]{3,2,1,0:T(8,128)}, f32[3,1,32,256]{3,2,1,0:T(8,128)}, u32[]{:S(2)}, u32[]{:S(2)}) collective-permute-start(f32[3,1,32,256]{3,2,1,0:T(8,128)} %get-tuple-element.44), channel_id=1, source_target_pairs={{0,112},{16,0},{32,16},{48,32},{64,48},{80,64},{96,80},{112,96},{1... | collective-permute-start | bytes 294920 | tf_op jit(solution)/shard_map/ppermute | solution.py:58
  30.5 2.1 %fusion.2 = (f32[3,16,31,256]{3,2,1,0:T(8,128)}, f32[3,16,31,256]{3,2,1,0:T(8,128)}) fusion(f32[2,16,32,256]{3,2,1,0:T(8,128)S(1)} %copy-done, f32[1,16,32,256]{3,2,1,0:T(8,128)S(1)} %get-tuple-element.23), kind=kLoop, calls=%fused_computation.24 | loop fusion | flops 761856 | bytes 4620288 | tf_op jit(solution)/shard_map/concatenate | solution.py:321
  32.7 2.0 %fusion.5 = (f32[3,15,32,256]{3,2,1,0:T(8,128)}, f32[3,15,32,256]{3,2,1,0:T(8,128)}) fusion(f32[2,16,32,256]{3,2,1,0:T(8,128)S(1)} %copy-done, f32[1,16,32,256]{3,2,1,0:T(8,128)S(1)} %get-tuple-element.23), kind=kLoop, calls=%fused_computation.29 | loop fusion | flops 737280 | bytes 4521984 | tf_op jit(solution)/shard_map/concatenate | solution.py:321
  34.7 5.0 %fusion.14 = f32[512,512]{1,0:T(8,128)} fusion(s32[512]{0:T(512)S(1)} %iota_add_fusion), kind=kLoop, calls=%fused_computation.40 | loop fusion | flops 2359296 | bytes 1050624 | tf_op jit(solution)/shard_map/sin | solution.py:75
  41.4 2.7 %reshape.199 = f32[8,16,2,16,32]{4,3,2,1,0:T(8,128)} reshape(f32[128,8,128]{2,1,0:T(8,128)} %all-to-all-done) | data formatting | bytes 1048576 | tf_op jit(solution)/shard_map/reshape | solution.py:111
  44.1 3.5 %fusion.7 = f32[2,128,2,16,32]{1,4,0,2,3:T(8,128)S(1)} fusion(f32[2,128,8,16,1,1]{1,3,2,0,5,4:T(8,128)} %bitcast.683, f32[8,16,2,16,32]{4,3,2,1,0:T(8,128)} %reshape.199), kind=kOutput, calls=%fused_computation.31 | convolution fusion | flops 201326592 | bytes 1703936 | tf_op jit(solution)/shard_map/rkax,abnxy->rknby/dot_general | solution.py:113
  60.9 2.6 %copy.304 = f32[128,2,18,34]{3,1,2,0:T(2,128)} copy(f32[128,2,18,34]{3,2,1,0:T(8,128)S(1)} %constant_dynamic-update-slice_fusion) | data formatting | bytes 1253376 | tf_op jit(solution)/shard_map/stack | solution.py:132
  63.5 5.3 %reshape.210 = f32[128,1,1224]{2,1,0:T(1,128)} reshape(f32[128,18,2,34]{3,2,1,0:T(2,128)} %bitcast.677) | data formatting | bytes 1253376
  68.8 5.7 %all-to-all-start.1 = ((f32[128,1,1224]{2,1,0:T(1,128)}), f32[128,1,1224]{2,1,0:T(1,128)}, u32[]{:S(2)}, u32[]{:S(2)}) async-start(f32[128,1,1224]{2,1,0:T(1,128)} %reshape.210), calls=%async_computation.1 | async-start | bytes 1310720 | tf_op jit(solution)/shard_map/all_to_all | solution.py:139
  74.5 2.9 %subtract_bitcast_fusion = (f32[16,32,256]{2,1,0:T(8,128)}, f32[1,16,32,256]{3,2,1,0:T(8,128)}, f32[16,32,256]{2,1,0:T(8,128)}, f32[1,16,32,256]{3,2,1,0:T(8,128)}) fusion(f32[1,16,32,256]{3,2,1,0:T(8,128)S(1)} %get-tuple-element.23, f32[2,16,32,256]{3,2,1,0:T(8,128)S(1)} %copy-done, f32[3,16,32,1]{3,2,1,0:T(8,128)} %get-tuple-element.51, ...), kind=kLoop, calls=%fused_computation.94 | loop fusion | flops 655360 | bytes 5249024 | tf_op jit(solution)/shard_map/mul | solution.py:298
  77.4 2.0 %subtract_bitcast_fusion.2 = (f32[16,32,256]{2,1,0:T(8,128)}, f32[1,16,32,256]{3,2,1,0:T(8,128)}) fusion(f32[3,16,31,256]{3,2,1,0:T(8,128)S(1)} %copy-done.3, f32[3,16,1,256]{3,2,1,0:T(1,128)} %collective-permute-done.7), kind=kLoop, calls=%fused_computation.96 | loop fusion | flops 262144 | bytes 2621440 | tf_op jit(solution)/shard_map/mul | solution.py:298
  79.4 1.9 %subtract_bitcast_fusion.3 = (f32[16,32,256]{2,1,0:T(8,128)}, f32[1,16,32,256]{3,2,1,0:T(8,128)}) fusion(f32[3,16,1,256]{3,2,1,0:T(1,128)} %collective-permute-done.6, f32[3,16,31,256]{3,2,1,0:T(8,128)S(1)} %copy-done.1), kind=kLoop, calls=%fused_computation.97 | loop fusion | flops 262144 | bytes 2621440 | tf_op jit(solution)/shard_map/mul | solution.py:297
  85.1 3.7 %all-to-all-done.1 = f32[128,1,1224]{2,1,0:T(1,128)} async-done(((f32[128,1,1224]{2,1,0:T(1,128)}), f32[128,1,1224]{2,1,0:T(1,128)}, u32[]{:S(2)}, u32[]{:S(2)}) %all-to-all-start.1) | async-done | bytes 626720 | tf_op jit(solution)/shard_map/all_to_all | solution.py:139
  89.3 3.3 %reduce = f32[128,1224]{1,0:T(8,128)S(1)} reduce(f32[128,1,1224]{2,1,0:T(1,128)} %all-to-all-done.1, f32[]{:T(128)} %broadcast.284), dimensions={1}, to_apply=%all_to_all.7.reduce_sub_computation | reduce | bytes 1253380 | tf_op jit(solution)/shard_map/all_to_all | solution.py:139
  92.6 3.6 %reshape.211 = f32[128,18,2,34]{3,2,1,0:T(2,128)} reshape(f32[128,1224]{1,0:T(8,128)S(1)} %reduce) | data formatting | bytes 1253376
  96.3 3.0 %copy.286 = f32[128,2,18,34]{3,1,0,2:T(2,128)S(1)} copy(f32[128,2,18,34]{3,1,2,0:T(2,128)} %bitcast.676) | data formatting | bytes 1253376 | tf_op jit(solution)/shard_map/all_to_all | solution.py:139
  99.3 2.0 %convolution_multiply_fusion.1 = f32[18,34,256]{2,1,0:T(8,128)S(1)} fusion(f32[256,18,34]{2,0,1:T(8,128)S(1)} %bitcast.675, f32[256,256]{1,0:T(8,128)S(1)} %fusion.42), kind=kOutput, calls=%fused_computation.34 | convolution fusion | flops 240804864 | bytes 1515520 | tf_op jit(solution)/shard_map/nz,nxy->xyz/dot_general | solution.py:141
  102.8 15.4 %shard_map.67 = (f32[19,16,32,256]{3,2,1,0:T(8,128)}, f32[3,16,32,256]{3,2,1,0:T(8,128)S(1)}, f32[10,16,1,256]{3,2,1,0:T(1,128)S(1)}) custom-call(f32[19,16,32,256]{3,2,1,0:T(8,128)} %pop_ref.1, f32[16,32,256]{2,1,0:T(8,128)S(1)} %convert_element_type.50.fluid_ref, f32[3,16,32,256]{3,2,1,0:T(8,128)S(1)} %pad_maximum_fusion.push_ref), custom_call_target="tpu_custom_call" | custom-call | tf_op jit(solution)/shard_map/pallas_call | solution.py:228
  123.1 5.1 %collective-permute-start.1 = (f32[5,32,256]{2,1,0:T(8,128)S(1)}, f32[5,32,256]{2,1,0:T(8,128)S(1)}, u32[]{:S(2)}, u32[]{:S(2)}) collective-permute-start(f32[5,32,256]{2,1,0:T(8,128)S(1)} %get-tuple-element.25), channel_id=1, source_target_pairs={{0,112},{16,0},{32,16},{48,32},{64,48},{80,64},{96,80},{112,96},{1... | collective-permute-start | bytes 491528 | tf_op jit(solution)/shard_map/ppermute | solution.py:348
  128.5 4.9 %multiply_add_fusion = f32[2,16,32,256]{3,2,1,0:T(8,128)} fusion(f32[2,16,32,256]{3,2,1,0:T(8,128)S(1)} %copy-done, f32[1,16,32,256]{3,2,1,0:T(8,128)S(1)} %get-tuple-element.23, f32[3,16,32,1]{3,2,1,0:T(8,128)S(1)} %copy-done.14, f32[3,16,32,1]{3,2,1,0:T(8,128)S(1)} %copy-done.13, f32[3,16,32,255]{3,2,1,0:T(8,128)S(1)} %copy-done.6, ...), kind=kLoop, calls=%fused_computation.63 | loop fusion | flops 13893632 | bytes 20977672 | tf_op jit(solution)/shard_map/add | solution.py:305
  135.7 4.1 %collective-permute-done.2 = f32[5,16,1,256]{3,2,1,0:T(1,128)S(1)} collective-permute-done((f32[5,16,1,256]{3,2,1,0:T(1,128)S(1)}, f32[5,16,1,256]{3,2,1,0:T(1,128)S(1)}, u32[]{:S(2)}, u32[]{:S(2)}) %collective-permute-start.2) | collective-permute-done | bytes 81952 | tf_op jit(solution)/shard_map/ppermute | solution.py:363
  140.7 2.6 %shard_map.68 = f32[19,16,32,256]{3,2,1,0:T(8,128)} custom-call(f32[10,1,32,256]{3,2,1,0:T(8,128)} %copy-done.24, f32[10,16,1,256]{3,2,1,0:T(1,128)} %pad_maximum_fusion.14.cols_ref, f32[19,16,32,256]{3,2,1,0:T(8,128)} %get-tuple-element.10.wrapped_hbm), custom_call_target="tpu_custom_call", output_to_operand_aliasing={{}: (2, {})} | custom-call | tf_op jit(solution)/shard_map/pallas_call | solution.py:273
  (252 shorter events, 38.1 us)
Async XLA Ops:
  0.6 16.6 %copy-start = (f32[2,16,32,256]{3,2,1,0:T(8,128)S(1)}, f32[2,16,32,256]{3,2,1,0:T(8,128)}, u32[]{:S(2)}) copy-start(f32[2,16,32,256]{3,2,1,0:T(8,128)} %param.5) | copy-start | bytes 3145732
  4.3 18.3 %copy-start.11 = (f32[16,32,256]{2,1,0:T(8,128)}, f32[16,32,256]{2,1,0:T(8,128)S(1)}, u32[]{:S(2)}) copy-start(f32[16,32,256]{2,1,0:T(8,128)S(1)} %fusion.39) | copy-start | bytes 1572868
  5.6 35.8 %all-to-all-start = ((f32[128,8,128]{2,1,0:T(8,128)}), f32[128,8,128]{2,1,0:T(8,128)}, u32[]{:S(2)}, u32[]{:S(2)}) async-start(f32[128,8,128]{2,1,0:T(8,128)} %reshape.198), calls=%async_computation | async-start | bytes 1048576 | tf_op jit(solution)/shard_map/all_to_all | solution.py:110
  18.0 59.4 %collective-permute-start.7 = (f32[3,16,1,256]{3,2,1,0:T(1,128)}, f32[3,16,1,256]{3,2,1,0:T(1,128)}, u32[]{:S(2)}, u32[]{:S(2)}) collective-permute-start(f32[3,16,1,256]{3,2,1,0:T(1,128)} %get-tuple-element.49), channel_id=1, source_target_pairs={{0,1},{1,2},{2,3},{3,4},{4,5},{5,6},{6,7},{7,8},{8,9},{9,10},{10,1... | collective-permute-start | bytes 147464 | tf_op jit(solution)/shard_map/ppermute | solution.py:57
  18.0 61.4 %collective-permute-start.6 = (f32[3,16,1,256]{3,2,1,0:T(1,128)}, f32[3,16,1,256]{3,2,1,0:T(1,128)}, u32[]{:S(2)}, u32[]{:S(2)}) collective-permute-start(f32[3,16,1,256]{3,2,1,0:T(1,128)} %get-tuple-element.48), channel_id=1, source_target_pairs={{0,15},{1,0},{2,1},{3,2},{4,3},{5,4},{6,5},{7,6},{8,7},{9,8},{10,9... | collective-permute-start | bytes 147464 | tf_op jit(solution)/shard_map/ppermute | solution.py:58
  22.6 58.8 %collective-permute-start.5 = (f32[3,1,32,256]{3,2,1,0:T(8,128)}, f32[3,1,32,256]{3,2,1,0:T(8,128)}, u32[]{:S(2)}, u32[]{:S(2)}) collective-permute-start(f32[3,1,32,256]{3,2,1,0:T(8,128)} %get-tuple-element.45), channel_id=1, source_target_pairs={{0,16},{16,32},{32,48},{48,64},{64,80},{80,96},{96,112},{112,0},{1... | collective-permute-start | bytes 294920 | tf_op jit(solution)/shard_map/ppermute | solution.py:57
  23.5 59.8 %collective-permute-start.4 = (f32[3,1,32,256]{3,2,1,0:T(8,128)}, f32[3,1,32,256]{3,2,1,0:T(8,128)}, u32[]{:S(2)}, u32[]{:S(2)}) collective-permute-start(f32[3,1,32,256]{3,2,1,0:T(8,128)} %get-tuple-element.44), channel_id=1, source_target_pairs={{0,112},{16,0},{32,16},{48,32},{64,48},{80,64},{96,80},{112,96},{1... | collective-permute-start | bytes 294920 | tf_op jit(solution)/shard_map/ppermute | solution.py:58
  30.5 43.9 %copy-start.5 = (f32[3,16,32,255]{3,2,1,0:T(8,128)}, f32[3,16,32,255]{3,2,1,0:T(8,128)S(1)}, u32[]{:S(2)}) copy-start(f32[3,16,32,255]{3,2,1,0:T(8,128)S(1)} %fusion.4) | copy-start | bytes 4700164
  68.8 20.0 %all-to-all-start.1 = ((f32[128,1,1224]{2,1,0:T(1,128)}), f32[128,1,1224]{2,1,0:T(1,128)}, u32[]{:S(2)}, u32[]{:S(2)}) async-start(f32[128,1,1224]{2,1,0:T(1,128)} %reshape.210), calls=%async_computation.1 | async-start | bytes 1310720 | tf_op jit(solution)/shard_map/all_to_all | solution.py:139
  102.7 25.6 %copy-start.6 = (f32[3,16,32,255]{3,2,1,0:T(8,128)S(1)}, f32[3,16,32,255]{3,2,1,0:T(8,128)}, u32[]{:S(2)}) copy-start(f32[3,16,32,255]{3,2,1,0:T(8,128)} %copy-done.5) | copy-start | bytes 4700164
  102.7 25.6 %copy-start.8 = (f32[3,15,32,256]{3,2,1,0:T(8,128)S(1)}, f32[3,15,32,256]{3,2,1,0:T(8,128)}, u32[]{:S(2)}) copy-start(f32[3,15,32,256]{3,2,1,0:T(8,128)} %get-tuple-element.42) | copy-start | bytes 4423684
  102.7 25.6 %copy-start.10 = (f32[3,15,32,256]{3,2,1,0:T(8,128)S(1)}, f32[3,15,32,256]{3,2,1,0:T(8,128)}, u32[]{:S(2)}) copy-start(f32[3,15,32,256]{3,2,1,0:T(8,128)} %get-tuple-element.43) | copy-start | bytes 4423684
  102.7 25.6 %copy-start.14 = (f32[3,16,32,1]{3,2,1,0:T(8,128)S(1)}, f32[3,16,32,1]{3,2,1,0:T(8,128)}, u32[]{:S(2)}) copy-start(f32[3,16,32,1]{3,2,1,0:T(8,128)} %get-tuple-element.51) | copy-start | bytes 18436
  102.7 25.6 %copy-start.17 = (f32[16,32,256]{2,1,0:T(8,128)S(1)}, f32[16,32,256]{2,1,0:T(8,128)}, u32[]{:S(2)}) copy-start(f32[16,32,256]{2,1,0:T(8,128)} %get-tuple-element.37) | copy-start | bytes 1572868
  102.8 25.6 %copy-start.18 = (f32[16,32,256]{2,1,0:T(8,128)S(1)}, f32[16,32,256]{2,1,0:T(8,128)}, u32[]{:S(2)}) copy-start(f32[16,32,256]{2,1,0:T(8,128)} %get-tuple-element.38) | copy-start | bytes 1572868
  102.8 25.6 %copy-start.19 = (f32[16,32,256]{2,1,0:T(8,128)S(1)}, f32[16,32,256]{2,1,0:T(8,128)}, u32[]{:S(2)}) copy-start(f32[16,32,256]{2,1,0:T(8,128)} %get-tuple-element.35) | copy-start | bytes 1572868
  102.8 25.6 %copy-start.20 = (f32[16,32,256]{2,1,0:T(8,128)S(1)}, f32[16,32,256]{2,1,0:T(8,128)}, u32[]{:S(2)}) copy-start(f32[16,32,256]{2,1,0:T(8,128)} %get-tuple-element.36) | copy-start | bytes 1572868
  102.8 25.6 %copy-start.21 = (f32[16,32,256]{2,1,0:T(8,128)S(1)}, f32[16,32,256]{2,1,0:T(8,128)}, u32[]{:S(2)}) copy-start(f32[16,32,256]{2,1,0:T(8,128)} %get-tuple-element.15) | copy-start | bytes 1572868
  118.2 10.3 %copy-start.13 = (f32[3,16,32,1]{3,2,1,0:T(8,128)S(1)}, f32[3,16,32,1]{3,2,1,0:T(8,128)}, u32[]{:S(2)}) copy-start(f32[3,16,32,1]{3,2,1,0:T(8,128)} %get-tuple-element.50) | copy-start | bytes 18436
  118.2 10.3 %copy-start.25 = (f32[2]{0:T(128)S(1)}, f32[2]{0:T(128)}, u32[]{:S(2)}) copy-start(f32[2]{0:T(128)} %constant.105.clone) | copy-start | bytes 28
  122.5 10.9 %collective-permute-start = (f32[5,32,256]{2,1,0:T(8,128)S(1)}, f32[5,32,256]{2,1,0:T(8,128)S(1)}, u32[]{:S(2)}, u32[]{:S(2)}) collective-permute-start(f32[5,32,256]{2,1,0:T(8,128)S(1)} %get-tuple-element.26), channel_id=1, source_target_pairs={{0,16},{16,32},{32,48},{48,64},{64,80},{80,96},{96,112},{112,0},{1... | collective-permute-start | bytes 491528 | tf_op jit(solution)/shard_map/ppermute | solution.py:348
  123.1 10.4 %collective-permute-start.1 = (f32[5,32,256]{2,1,0:T(8,128)S(1)}, f32[5,32,256]{2,1,0:T(8,128)S(1)}, u32[]{:S(2)}, u32[]{:S(2)}) collective-permute-start(f32[5,32,256]{2,1,0:T(8,128)S(1)} %get-tuple-element.25), channel_id=1, source_target_pairs={{0,112},{16,0},{32,16},{48,32},{64,48},{80,64},{96,80},{112,96},{1... | collective-permute-start | bytes 491528 | tf_op jit(solution)/shard_map/ppermute | solution.py:348
  133.6 2.1 %collective-permute-start.3 = (f32[5,16,1,256]{3,2,1,0:T(1,128)S(1)}, f32[5,16,1,256]{3,2,1,0:T(1,128)S(1)}, u32[]{:S(2)}, u32[]{:S(2)}) collective-permute-start(f32[5,16,1,256]{3,2,1,0:T(1,128)S(1)} %pad_maximum_fusion.17), channel_id=1, source_target_pairs={{0,15},{1,0},{2,1},{3,2},{4,3},{5,4},{6,5},{7,6},{8,7},{9,8},{10,9... | collective-permute-start | bytes 245768 | tf_op jit(solution)/shard_map/ppermute | solution.py:363
  133.8 6.0 %collective-permute-start.2 = (f32[5,16,1,256]{3,2,1,0:T(1,128)S(1)}, f32[5,16,1,256]{3,2,1,0:T(1,128)S(1)}, u32[]{:S(2)}, u32[]{:S(2)}) collective-permute-start(f32[5,16,1,256]{3,2,1,0:T(1,128)S(1)} %pad_maximum_fusion.16), channel_id=1, source_target_pairs={{0,1},{1,2},{2,3},{3,4},{4,5},{5,6},{6,7},{7,8},{8,9},{9,10},{10,1... | collective-permute-start | bytes 245768 | tf_op jit(solution)/shard_map/ppermute | solution.py:363
  (12 other events, 55.7 us)

commit v2 on v0

--- a/solution.py
+++ b/solution.py
@@ -224,7 +224,7 @@
 
 def stream_call(populations, distribution_tuple, push):
     entries, len_local, wid_local, depth = populations.shape
-    rows = 2
+    rows = 4
     big = lambda n: pl.BlockSpec((n, rows, wid_local, depth), lambda i: (0, i, 0, 0))
     return pl.pallas_call(
         stream_kernel,

time: 143 us -> 143 us (level)
  no operation moved by 1% of the time
where the time goes in v2:
time: 143 us; the launch traced here: 142 us
  other arithmetic  40.7 us (28%)
  starting transfers between devices  33.4 us (23%)
  local copies, waits for them, and re-layouts  30.4 us (21%)
  Pallas kernels  17.3 us (12%)
  matrix products  9.28 us (6%)
  waiting for transfers between devices  9.12 us (6%)
  between operations  1.55 us (1%)
    unnamed x166, local copies, waits for them, and re-layouts  19.8 us
    pallas_call x1, Pallas kernels, stream_call(): pl.pallas_call(stream_kernel, grid=(len_local // rows,), in_specs=[big(en...  14.7 us
    all_to_all x1, starting transfers between devices, solve_potential(): plane = lax.all_to_all(sectioned, ('gx', 'gy'), 0, 0, tiled=True)  11.7 us
    ppermute x2, starting transfers between devices, halos(): lax.ppermute(lax.slice_in_dim(block, 0, 1, axis=dim), axis, ring(axis, -1))  8.61 us
    concatenate x6, other arithmetic, body(): ionic = jnp.concatenate([ions, distribution_tuple[None]], axis=0)  7.52 us
    mul x3, other arithmetic, drift_diffuse(): low_val = lower[2:3] * lower[:2] + (1.0 - lower[2:3]) * conc  6.73 us
    sin x2, other arithmetic, sine_table(): return jnp.sin(product.astype(jnp.float32) * (math.pi / (length + 1)))  6.11 us
    all_to_all x1, starting transfers between devices, solve_potential(): back = lax.all_to_all(blocks, ('gx', 'gy'), 0, 0, tiled=True)  5.9 us
  transfers between devices with their start and end apart: 10, of which 3 were waited for; matrix products, arithmetic and copies ran while one was open for 36% of the time, Pallas kernels for 0%

profile of v2, /device:TPU:0, one launch (start us, length us, event | category | flops | bytes accessed | tf_op | source)
XLA Modules:
  0.0 141.8 jit_solution(4482756603786274062)
XLA Ops:
  3.2 5.0 %fusion.14 = f32[512,512]{1,0:T(8,128)} fusion(s32[512]{0:T(512)S(1)} %iota_add_fusion), kind=kLoop, calls=%fused_computation.40 | loop fusion | flops 2359296 | bytes 1050624 | tf_op jit(solution)/shard_map/sin | solution.py:75
  10.3 11.7 %all-to-all-start = ((f32[128,8,128]{2,1,0:T(8,128)}), f32[128,8,128]{2,1,0:T(8,128)}, u32[]{:S(2)}, u32[]{:S(2)}) async-start(f32[128,8,128]{2,1,0:T(8,128)} %reshape.198), calls=%async_computation | async-start | bytes 1048576 | tf_op jit(solution)/shard_map/all_to_all | solution.py:111
  22.7 3.9 %collective-permute-start.6 = (f32[3,16,1,256]{3,2,1,0:T(1,128)}, f32[3,16,1,256]{3,2,1,0:T(1,128)}, u32[]{:S(2)}, u32[]{:S(2)}) collective-permute-start(f32[3,16,1,256]{3,2,1,0:T(1,128)} %get-tuple-element.50), channel_id=1, source_target_pairs={{0,15},{1,0},{2,1},{3,2},{4,3},{5,4},{6,5},{7,6},{8,7},{9,8},{10,9... | collective-permute-start | bytes 147464 | tf_op jit(solution)/shard_map/ppermute | solution.py:58
  28.2 4.8 %collective-permute-start.4 = (f32[3,1,32,256]{3,2,1,0:T(8,128)}, f32[3,1,32,256]{3,2,1,0:T(8,128)}, u32[]{:S(2)}, u32[]{:S(2)}) collective-permute-start(f32[3,1,32,256]{3,2,1,0:T(8,128)} %get-tuple-element.46), channel_id=1, source_target_pairs={{0,112},{16,0},{32,16},{48,32},{64,48},{80,64},{96,80},{112,96},{1... | collective-permute-start | bytes 294920 | tf_op jit(solution)/shard_map/ppermute | solution.py:58
  35.0 2.1 %fusion.2 = (f32[3,16,31,256]{3,2,1,0:T(8,128)}, f32[3,16,31,256]{3,2,1,0:T(8,128)}) fusion(f32[2,16,32,256]{3,2,1,0:T(8,128)S(1)} %copy-done, f32[1,16,32,256]{3,2,1,0:T(8,128)S(1)} %get-tuple-element.25), kind=kLoop, calls=%fused_computation.24 | loop fusion | flops 761856 | bytes 4620288 | tf_op jit(solution)/shard_map/concatenate | solution.py:322
  37.1 2.0 %fusion.5 = (f32[3,15,32,256]{3,2,1,0:T(8,128)}, f32[3,15,32,256]{3,2,1,0:T(8,128)}) fusion(f32[2,16,32,256]{3,2,1,0:T(8,128)S(1)} %copy-done, f32[1,16,32,256]{3,2,1,0:T(8,128)S(1)} %get-tuple-element.25), kind=kLoop, calls=%fused_computation.29 | loop fusion | flops 737280 | bytes 4521984 | tf_op jit(solution)/shard_map/concatenate | solution.py:322
  40.2 2.7 %reshape.199 = f32[8,16,2,16,32]{4,3,2,1,0:T(8,128)} reshape(f32[128,8,128]{2,1,0:T(8,128)} %all-to-all-done) | data formatting | bytes 1048576 | tf_op jit(solution)/shard_map/reshape | solution.py:112
  42.9 3.5 %fusion.7 = f32[2,128,2,16,32]{1,4,0,2,3:T(8,128)S(1)} fusion(f32[2,128,8,16,1,1]{1,3,2,0,5,4:T(8,128)} %bitcast.683, f32[8,16,2,16,32]{4,3,2,1,0:T(8,128)} %reshape.199), kind=kOutput, calls=%fused_computation.31 | convolution fusion | flops 201326592 | bytes 1703936 | tf_op jit(solution)/shard_map/rkax,abnxy->rknby/dot_general | solution.py:114
  59.7 2.6 %copy.304 = f32[128,2,18,34]{3,1,2,0:T(2,128)} copy(f32[128,2,18,34]{3,2,1,0:T(8,128)S(1)} %constant_dynamic-update-slice_fusion) | data formatting | bytes 1253376 | tf_op jit(solution)/shard_map/stack | solution.py:133
  62.3 5.3 %reshape.210 = f32[128,1,1224]{2,1,0:T(1,128)} reshape(f32[128,18,2,34]{3,2,1,0:T(2,128)} %bitcast.677) | data formatting | bytes 1253376
  67.5 5.9 %all-to-all-start.1 = ((f32[128,1,1224]{2,1,0:T(1,128)}), f32[128,1,1224]{2,1,0:T(1,128)}, u32[]{:S(2)}, u32[]{:S(2)}) async-start(f32[128,1,1224]{2,1,0:T(1,128)} %reshape.210), calls=%async_computation.1 | async-start | bytes 1310720 | tf_op jit(solution)/shard_map/all_to_all | solution.py:140
  73.5 2.9 %subtract_bitcast_fusion = (f32[16,32,256]{2,1,0:T(8,128)}, f32[1,16,32,256]{3,2,1,0:T(8,128)}, f32[16,32,256]{2,1,0:T(8,128)}, f32[1,16,32,256]{3,2,1,0:T(8,128)}) fusion(f32[1,16,32,256]{3,2,1,0:T(8,128)S(1)} %get-tuple-element.25, f32[2,16,32,256]{3,2,1,0:T(8,128)S(1)} %copy-done, f32[3,16,32,1]{3,2,1,0:T(8,128)} %get-tuple-element.53, ...), kind=kLoop, calls=%fused_computation.94 | loop fusion | flops 655360 | bytes 5249024 | tf_op jit(solution)/shard_map/mul | solution.py:299
  76.4 2.0 %subtract_bitcast_fusion.2 = (f32[16,32,256]{2,1,0:T(8,128)}, f32[1,16,32,256]{3,2,1,0:T(8,128)}) fusion(f32[3,16,31,256]{3,2,1,0:T(8,128)S(1)} %copy-done.3, f32[3,16,1,256]{3,2,1,0:T(1,128)} %collective-permute-done.7), kind=kLoop, calls=%fused_computation.96 | loop fusion | flops 262144 | bytes 2621440 | tf_op jit(solution)/shard_map/mul | solution.py:299
  78.4 1.9 %subtract_bitcast_fusion.3 = (f32[16,32,256]{2,1,0:T(8,128)}, f32[1,16,32,256]{3,2,1,0:T(8,128)}) fusion(f32[3,16,1,256]{3,2,1,0:T(1,128)} %collective-permute-done.6, f32[3,16,31,256]{3,2,1,0:T(8,128)S(1)} %copy-done.1), kind=kLoop, calls=%fused_computation.97 | loop fusion | flops 262144 | bytes 2621440 | tf_op jit(solution)/shard_map/mul | solution.py:298
  84.1 3.7 %all-to-all-done.1 = f32[128,1,1224]{2,1,0:T(1,128)} async-done(((f32[128,1,1224]{2,1,0:T(1,128)}), f32[128,1,1224]{2,1,0:T(1,128)}, u32[]{:S(2)}, u32[]{:S(2)}) %all-to-all-start.1) | async-done | bytes 626720 | tf_op jit(solution)/shard_map/all_to_all | solution.py:140
  88.3 3.3 %reduce = f32[128,1224]{1,0:T(8,128)S(1)} reduce(f32[128,1,1224]{2,1,0:T(1,128)} %all-to-all-done.1, f32[]{:T(128)} %broadcast.284), dimensions={1}, to_apply=%all_to_all.7.reduce_sub_computation | reduce | bytes 1253380 | tf_op jit(solution)/shard_map/all_to_all | solution.py:140
  91.6 3.6 %reshape.211 = f32[128,18,2,34]{3,2,1,0:T(2,128)} reshape(f32[128,1224]{1,0:T(8,128)S(1)} %reduce) | data formatting | bytes 1253376
  95.3 3.0 %copy.286 = f32[128,2,18,34]{3,1,0,2:T(2,128)S(1)} copy(f32[128,2,18,34]{3,1,2,0:T(2,128)} %bitcast.676) | data formatting | bytes 1253376 | tf_op jit(solution)/shard_map/all_to_all | solution.py:140
  98.3 2.0 %convolution_multiply_fusion.1 = f32[18,34,256]{2,1,0:T(8,128)S(1)} fusion(f32[256,18,34]{2,0,1:T(8,128)S(1)} %bitcast.675, f32[256,256]{1,0:T(8,128)S(1)} %fusion.42), kind=kOutput, calls=%fused_computation.34 | convolution fusion | flops 240804864 | bytes 1515520 | tf_op jit(solution)/shard_map/nz,nxy->xyz/dot_general | solution.py:142
  101.8 14.7 %shard_map.67 = (f32[19,16,32,256]{3,2,1,0:T(8,128)}, f32[3,16,32,256]{3,2,1,0:T(8,128)S(1)}, f32[10,16,1,256]{3,2,1,0:T(1,128)S(1)}) custom-call(f32[19,16,32,256]{3,2,1,0:T(8,128)} %pop_ref.1, f32[16,32,256]{2,1,0:T(8,128)S(1)} %convert_element_type.50.fluid_ref, f32[3,16,32,256]{3,2,1,0:T(8,128)S(1)} %pad_maximum_fusion.push_ref), custom_call_target="tpu_custom_call" | custom-call | tf_op jit(solution)/shard_map/pallas_call | solution.py:229
  121.4 5.1 %collective-permute-start.1 = (f32[5,32,256]{2,1,0:T(8,128)S(1)}, f32[5,32,256]{2,1,0:T(8,128)S(1)}, u32[]{:S(2)}, u32[]{:S(2)}) collective-permute-start(f32[5,32,256]{2,1,0:T(8,128)S(1)} %get-tuple-element.27), channel_id=1, source_target_pairs={{0,112},{16,0},{32,16},{48,32},{64,48},{80,64},{96,80},{112,96},{1... | collective-permute-start | bytes 491528 | tf_op jit(solution)/shard_map/ppermute | solution.py:349
  126.8 4.9 %multiply_add_fusion = f32[2,16,32,256]{3,2,1,0:T(8,128)} fusion(f32[2,16,32,256]{3,2,1,0:T(8,128)S(1)} %copy-done, f32[1,16,32,256]{3,2,1,0:T(8,128)S(1)} %get-tuple-element.25, f32[3,16,32,1]{3,2,1,0:T(8,128)S(1)} %copy-done.14, f32[3,16,32,1]{3,2,1,0:T(8,128)S(1)} %copy-done.13, f32[3,16,32,255]{3,2,1,0:T(8,128)S(1)} %copy-done.6, ...), kind=kLoop, calls=%fused_computation.63 | loop fusion | flops 13893632 | bytes 20977672 | tf_op jit(solution)/shard_map/add | solution.py:306
  134.1 4.1 %collective-permute-done.2 = f32[5,16,1,256]{3,2,1,0:T(1,128)S(1)} collective-permute-done((f32[5,16,1,256]{3,2,1,0:T(1,128)S(1)}, f32[5,16,1,256]{3,2,1,0:T(1,128)S(1)}, u32[]{:S(2)}, u32[]{:S(2)}) %collective-permute-start.2) | collective-permute-done | bytes 81952 | tf_op jit(solution)/shard_map/ppermute | solution.py:364
  139.1 2.6 %shard_map.68 = f32[19,16,32,256]{3,2,1,0:T(8,128)} custom-call(f32[10,1,32,256]{3,2,1,0:T(8,128)} %copy-done.24, f32[10,16,1,256]{3,2,1,0:T(1,128)} %pad_maximum_fusion.14.cols_ref, f32[19,16,32,256]{3,2,1,0:T(8,128)} %get-tuple-element.12.wrapped_hbm), custom_call_target="tpu_custom_call", output_to_operand_aliasing={{}: (2, {})} | custom-call | tf_op jit(solution)/shard_map/pallas_call | solution.py:274
  (252 shorter events, 36.9 us)
Async XLA Ops:
  9.0 18.3 %copy-start.11 = (f32[16,32,256]{2,1,0:T(8,128)}, f32[16,32,256]{2,1,0:T(8,128)S(1)}, u32[]{:S(2)}) copy-start(f32[16,32,256]{2,1,0:T(8,128)S(1)} %fusion.39) | copy-start | bytes 1572868
  10.3 29.9 %all-to-all-start = ((f32[128,8,128]{2,1,0:T(8,128)}), f32[128,8,128]{2,1,0:T(8,128)}, u32[]{:S(2)}, u32[]{:S(2)}) async-start(f32[128,8,128]{2,1,0:T(8,128)} %reshape.198), calls=%async_computation | async-start | bytes 1048576 | tf_op jit(solution)/shard_map/all_to_all | solution.py:111
  22.7 53.7 %collective-permute-start.7 = (f32[3,16,1,256]{3,2,1,0:T(1,128)}, f32[3,16,1,256]{3,2,1,0:T(1,128)}, u32[]{:S(2)}, u32[]{:S(2)}) collective-permute-start(f32[3,16,1,256]{3,2,1,0:T(1,128)} %get-tuple-element.51), channel_id=1, source_target_pairs={{0,1},{1,2},{2,3},{3,4},{4,5},{5,6},{6,7},{7,8},{8,9},{9,10},{10,1... | collective-permute-start | bytes 147464 | tf_op jit(solution)/shard_map/ppermute | solution.py:57
  22.7 55.6 %collective-permute-start.6 = (f32[3,16,1,256]{3,2,1,0:T(1,128)}, f32[3,16,1,256]{3,2,1,0:T(1,128)}, u32[]{:S(2)}, u32[]{:S(2)}) collective-permute-start(f32[3,16,1,256]{3,2,1,0:T(1,128)} %get-tuple-element.50), channel_id=1, source_target_pairs={{0,15},{1,0},{2,1},{3,2},{4,3},{5,4},{6,5},{7,6},{8,7},{9,8},{10,9... | collective-permute-start | bytes 147464 | tf_op jit(solution)/shard_map/ppermute | solution.py:58
  27.3 53.0 %collective-permute-start.5 = (f32[3,1,32,256]{3,2,1,0:T(8,128)}, f32[3,1,32,256]{3,2,1,0:T(8,128)}, u32[]{:S(2)}, u32[]{:S(2)}) collective-permute-start(f32[3,1,32,256]{3,2,1,0:T(8,128)} %get-tuple-element.47), channel_id=1, source_target_pairs={{0,16},{16,32},{32,48},{48,64},{64,80},{80,96},{96,112},{112,0},{1... | collective-permute-start | bytes 294920 | tf_op jit(solution)/shard_map/ppermute | solution.py:57
  28.2 54.0 %collective-permute-start.4 = (f32[3,1,32,256]{3,2,1,0:T(8,128)}, f32[3,1,32,256]{3,2,1,0:T(8,128)}, u32[]{:S(2)}, u32[]{:S(2)}) collective-permute-start(f32[3,1,32,256]{3,2,1,0:T(8,128)} %get-tuple-element.46), channel_id=1, source_target_pairs={{0,112},{16,0},{32,16},{48,32},{64,48},{80,64},{96,80},{112,96},{1... | collective-permute-start | bytes 294920 | tf_op jit(solution)/shard_map/ppermute | solution.py:58
  35.0 38.5 %copy-start.5 = (f32[3,16,32,255]{3,2,1,0:T(8,128)}, f32[3,16,32,255]{3,2,1,0:T(8,128)S(1)}, u32[]{:S(2)}) copy-start(f32[3,16,32,255]{3,2,1,0:T(8,128)S(1)} %fusion.4) | copy-start | bytes 4700164
  67.5 20.3 %all-to-all-start.1 = ((f32[128,1,1224]{2,1,0:T(1,128)}), f32[128,1,1224]{2,1,0:T(1,128)}, u32[]{:S(2)}, u32[]{:S(2)}) async-start(f32[128,1,1224]{2,1,0:T(1,128)} %reshape.210), calls=%async_computation.1 | async-start | bytes 1310720 | tf_op jit(solution)/shard_map/all_to_all | solution.py:140
  101.7 25.0 %copy-start.6 = (f32[3,16,32,255]{3,2,1,0:T(8,128)S(1)}, f32[3,16,32,255]{3,2,1,0:T(8,128)}, u32[]{:S(2)}) copy-start(f32[3,16,32,255]{3,2,1,0:T(8,128)} %copy-done.5) | copy-start | bytes 4700164
  101.7 25.0 %copy-start.8 = (f32[3,15,32,256]{3,2,1,0:T(8,128)S(1)}, f32[3,15,32,256]{3,2,1,0:T(8,128)}, u32[]{:S(2)}) copy-start(f32[3,15,32,256]{3,2,1,0:T(8,128)} %get-tuple-element.44) | copy-start | bytes 4423684
  101.7 25.0 %copy-start.10 = (f32[3,15,32,256]{3,2,1,0:T(8,128)S(1)}, f32[3,15,32,256]{3,2,1,0:T(8,128)}, u32[]{:S(2)}) copy-start(f32[3,15,32,256]{3,2,1,0:T(8,128)} %get-tuple-element.45) | copy-start | bytes 4423684
  101.7 25.0 %copy-start.14 = (f32[3,16,32,1]{3,2,1,0:T(8,128)S(1)}, f32[3,16,32,1]{3,2,1,0:T(8,128)}, u32[]{:S(2)}) copy-start(f32[3,16,32,1]{3,2,1,0:T(8,128)} %get-tuple-element.53) | copy-start | bytes 18436
  101.7 25.0 %copy-start.17 = (f32[16,32,256]{2,1,0:T(8,128)S(1)}, f32[16,32,256]{2,1,0:T(8,128)}, u32[]{:S(2)}) copy-start(f32[16,32,256]{2,1,0:T(8,128)} %get-tuple-element.39) | copy-start | bytes 1572868
  101.7 25.0 %copy-start.18 = (f32[16,32,256]{2,1,0:T(8,128)S(1)}, f32[16,32,256]{2,1,0:T(8,128)}, u32[]{:S(2)}) copy-start(f32[16,32,256]{2,1,0:T(8,128)} %get-tuple-element.40) | copy-start | bytes 1572868
  101.8 25.0 %copy-start.19 = (f32[16,32,256]{2,1,0:T(8,128)S(1)}, f32[16,32,256]{2,1,0:T(8,128)}, u32[]{:S(2)}) copy-start(f32[16,32,256]{2,1,0:T(8,128)} %get-tuple-element.37) | copy-start | bytes 1572868
  101.8 25.0 %copy-start.20 = (f32[16,32,256]{2,1,0:T(8,128)S(1)}, f32[16,32,256]{2,1,0:T(8,128)}, u32[]{:S(2)}) copy-start(f32[16,32,256]{2,1,0:T(8,128)} %get-tuple-element.38) | copy-start | bytes 1572868
  101.8 25.0 %copy-start.21 = (f32[16,32,256]{2,1,0:T(8,128)S(1)}, f32[16,32,256]{2,1,0:T(8,128)}, u32[]{:S(2)}) copy-start(f32[16,32,256]{2,1,0:T(8,128)} %get-tuple-element.17) | copy-start | bytes 1572868
  116.5 10.3 %copy-start.4 = (f32[3,16,31,256]{3,2,1,0:T(8,128)S(1)}, f32[3,16,31,256]{3,2,1,0:T(8,128)}, u32[]{:S(2)}) copy-start(f32[3,16,31,256]{3,2,1,0:T(8,128)} %get-tuple-element.49) | copy-start | bytes 4571140
  116.5 10.3 %copy-start.13 = (f32[3,16,32,1]{3,2,1,0:T(8,128)S(1)}, f32[3,16,32,1]{3,2,1,0:T(8,128)}, u32[]{:S(2)}) copy-start(f32[3,16,32,1]{3,2,1,0:T(8,128)} %get-tuple-element.52) | copy-start | bytes 18436
  116.5 10.3 %copy-start.25 = (f32[2]{0:T(128)S(1)}, f32[2]{0:T(128)}, u32[]{:S(2)}) copy-start(f32[2]{0:T(128)} %constant.105.clone) | copy-start | bytes 28
  120.9 10.9 %collective-permute-start = (f32[5,32,256]{2,1,0:T(8,128)S(1)}, f32[5,32,256]{2,1,0:T(8,128)S(1)}, u32[]{:S(2)}, u32[]{:S(2)}) collective-permute-start(f32[5,32,256]{2,1,0:T(8,128)S(1)} %get-tuple-element.28), channel_id=1, source_target_pairs={{0,16},{16,32},{32,48},{48,64},{64,80},{80,96},{96,112},{112,0},{1... | collective-permute-start | bytes 491528 | tf_op jit(solution)/shard_map/ppermute | solution.py:349
  121.4 10.4 %collective-permute-start.1 = (f32[5,32,256]{2,1,0:T(8,128)S(1)}, f32[5,32,256]{2,1,0:T(8,128)S(1)}, u32[]{:S(2)}, u32[]{:S(2)}) collective-permute-start(f32[5,32,256]{2,1,0:T(8,128)S(1)} %get-tuple-element.27), channel_id=1, source_target_pairs={{0,112},{16,0},{32,16},{48,32},{64,48},{80,64},{96,80},{112,96},{1... | collective-permute-start | bytes 491528 | tf_op jit(solution)/shard_map/ppermute | solution.py:349
  132.0 2.1 %collective-permute-start.3 = (f32[5,16,1,256]{3,2,1,0:T(1,128)S(1)}, f32[5,16,1,256]{3,2,1,0:T(1,128)S(1)}, u32[]{:S(2)}, u32[]{:S(2)}) collective-permute-start(f32[5,16,1,256]{3,2,1,0:T(1,128)S(1)} %pad_maximum_fusion.17), channel_id=1, source_target_pairs={{0,15},{1,0},{2,1},{3,2},{4,3},{5,4},{6,5},{7,6},{8,7},{9,8},{10,9... | collective-permute-start | bytes 245768 | tf_op jit(solution)/shard_map/ppermute | solution.py:364
  132.2 6.0 %collective-permute-start.2 = (f32[5,16,1,256]{3,2,1,0:T(1,128)S(1)}, f32[5,16,1,256]{3,2,1,0:T(1,128)S(1)}, u32[]{:S(2)}, u32[]{:S(2)}) collective-permute-start(f32[5,16,1,256]{3,2,1,0:T(1,128)S(1)} %pad_maximum_fusion.16), channel_id=1, source_target_pairs={{0,1},{1,2},{2,3},{3,4},{4,5},{5,6},{6,7},{7,8},{8,9},{9,10},{10,1... | collective-permute-start | bytes 245768 | tf_op jit(solution)/shard_map/ppermute | solution.py:364
  (12 other events, 53.6 us)

commit v3 on v2

--- a/solution.py
+++ b/solution.py
@@ -224,7 +224,7 @@
 
 def stream_call(populations, distribution_tuple, push):
     entries, len_local, wid_local, depth = populations.shape
-    rows = 4
+    rows = 8
     big = lambda n: pl.BlockSpec((n, rows, wid_local, depth), lambda i: (0, i, 0, 0))
     return pl.pallas_call(
         stream_kernel,

time: 143 us -> 143 us (level)
  no operation moved by 1% of the time
where the time goes in v3:
time: 143 us; the launch traced here: 142 us
  other arithmetic  40.7 us (28%)
  starting transfers between devices  33.4 us (23%)
  local copies, waits for them, and re-layouts  30.4 us (21%)
  Pallas kernels  17.9 us (13%)
  matrix products  9.28 us (6%)
  waiting for transfers between devices  9.12 us (6%)
  between operations  1.55 us (1%)
    unnamed x166, local copies, waits for them, and re-layouts  19.8 us
    pallas_call x1, Pallas kernels, stream_call(): pl.pallas_call(stream_kernel, grid=(len_local // rows,), in_specs=[big(en...  15.3 us
    all_to_all x1, starting transfers between devices, solve_potential(): plane = lax.all_to_all(sectioned, ('gx', 'gy'), 0, 0, tiled=True)  11.7 us
    ppermute x2, starting transfers between devices, halos(): lax.ppermute(lax.slice_in_dim(block, 0, 1, axis=dim), axis, ring(axis, -1))  8.61 us
    concatenate x6, other arithmetic, body(): ionic = jnp.concatenate([ions, distribution_tuple[None]], axis=0)  7.52 us
    mul x3, other arithmetic, drift_diffuse(): low_val = lower[2:3] * lower[:2] + (1.0 - lower[2:3]) * conc  6.73 us
    sin x2, other arithmetic, sine_table(): return jnp.sin(product.astype(jnp.float32) * (math.pi / (length + 1)))  6.11 us
    all_to_all x1, starting transfers between devices, solve_potential(): back = lax.all_to_all(blocks, ('gx', 'gy'), 0, 0, tiled=True)  5.9 us
  transfers between devices with their start and end apart: 10, of which 3 were waited for; matrix products, arithmetic and copies ran while one was open for 36% of the time, Pallas kernels for 0%

profile of v3, /device:TPU:0, one launch (start us, length us, event | category | flops | bytes accessed | tf_op | source)
XLA Modules:
  0.0 142.4 jit_solution(882547793776691434)
XLA Ops:
  3.2 5.0 %fusion.14 = f32[512,512]{1,0:T(8,128)} fusion(s32[512]{0:T(512)S(1)} %iota_add_fusion), kind=kLoop, calls=%fused_computation.40 | loop fusion | flops 2359296 | bytes 1050624 | tf_op jit(solution)/shard_map/sin | solution.py:75
  10.3 11.7 %all-to-all-start = ((f32[128,8,128]{2,1,0:T(8,128)}), f32[128,8,128]{2,1,0:T(8,128)}, u32[]{:S(2)}, u32[]{:S(2)}) async-start(f32[128,8,128]{2,1,0:T(8,128)} %reshape.198), calls=%async_computation | async-start | bytes 1048576 | tf_op jit(solution)/shard_map/all_to_all | solution.py:111
  22.7 3.9 %collective-permute-start.6 = (f32[3,16,1,256]{3,2,1,0:T(1,128)}, f32[3,16,1,256]{3,2,1,0:T(1,128)}, u32[]{:S(2)}, u32[]{:S(2)}) collective-permute-start(f32[3,16,1,256]{3,2,1,0:T(1,128)} %get-tuple-element.50), channel_id=1, source_target_pairs={{0,15},{1,0},{2,1},{3,2},{4,3},{5,4},{6,5},{7,6},{8,7},{9,8},{10,9... | collective-permute-start | bytes 147464 | tf_op jit(solution)/shard_map/ppermute | solution.py:58
  28.2 4.8 %collective-permute-start.4 = (f32[3,1,32,256]{3,2,1,0:T(8,128)}, f32[3,1,32,256]{3,2,1,0:T(8,128)}, u32[]{:S(2)}, u32[]{:S(2)}) collective-permute-start(f32[3,1,32,256]{3,2,1,0:T(8,128)} %get-tuple-element.46), channel_id=1, source_target_pairs={{0,112},{16,0},{32,16},{48,32},{64,48},{80,64},{96,80},{112,96},{1... | collective-permute-start | bytes 294920 | tf_op jit(solution)/shard_map/ppermute | solution.py:58
  35.0 2.1 %fusion.2 = (f32[3,16,31,256]{3,2,1,0:T(8,128)}, f32[3,16,31,256]{3,2,1,0:T(8,128)}) fusion(f32[2,16,32,256]{3,2,1,0:T(8,128)S(1)} %copy-done, f32[1,16,32,256]{3,2,1,0:T(8,128)S(1)} %get-tuple-element.25), kind=kLoop, calls=%fused_computation.24 | loop fusion | flops 761856 | bytes 4620288 | tf_op jit(solution)/shard_map/concatenate | solution.py:322
  37.1 2.0 %fusion.5 = (f32[3,15,32,256]{3,2,1,0:T(8,128)}, f32[3,15,32,256]{3,2,1,0:T(8,128)}) fusion(f32[2,16,32,256]{3,2,1,0:T(8,128)S(1)} %copy-done, f32[1,16,32,256]{3,2,1,0:T(8,128)S(1)} %get-tuple-element.25), kind=kLoop, calls=%fused_computation.29 | loop fusion | flops 737280 | bytes 4521984 | tf_op jit(solution)/shard_map/concatenate | solution.py:322
  40.2 2.7 %reshape.199 = f32[8,16,2,16,32]{4,3,2,1,0:T(8,128)} reshape(f32[128,8,128]{2,1,0:T(8,128)} %all-to-all-done) | data formatting | bytes 1048576 | tf_op jit(solution)/shard_map/reshape | solution.py:112
  42.9 3.5 %fusion.7 = f32[2,128,2,16,32]{1,4,0,2,3:T(8,128)S(1)} fusion(f32[2,128,8,16,1,1]{1,3,2,0,5,4:T(8,128)} %bitcast.683, f32[8,16,2,16,32]{4,3,2,1,0:T(8,128)} %reshape.199), kind=kOutput, calls=%fused_computation.31 | convolution fusion | flops 201326592 | bytes 1703936 | tf_op jit(solution)/shard_map/rkax,abnxy->rknby/dot_general | solution.py:114
  59.7 2.6 %copy.304 = f32[128,2,18,34]{3,1,2,0:T(2,128)} copy(f32[128,2,18,34]{3,2,1,0:T(8,128)S(1)} %constant_dynamic-update-slice_fusion) | data formatting | bytes 1253376 | tf_op jit(solution)/shard_map/stack | solution.py:133
  62.3 5.3 %reshape.210 = f32[128,1,1224]{2,1,0:T(1,128)} reshape(f32[128,18,2,34]{3,2,1,0:T(2,128)} %bitcast.677) | data formatting | bytes 1253376
  67.5 5.9 %all-to-all-start.1 = ((f32[128,1,1224]{2,1,0:T(1,128)}), f32[128,1,1224]{2,1,0:T(1,128)}, u32[]{:S(2)}, u32[]{:S(2)}) async-start(f32[128,1,1224]{2,1,0:T(1,128)} %reshape.210), calls=%async_computation.1 | async-start | bytes 1310720 | tf_op jit(solution)/shard_map/all_to_all | solution.py:140
  73.5 2.9 %subtract_bitcast_fusion = (f32[16,32,256]{2,1,0:T(8,128)}, f32[1,16,32,256]{3,2,1,0:T(8,128)}, f32[16,32,256]{2,1,0:T(8,128)}, f32[1,16,32,256]{3,2,1,0:T(8,128)}) fusion(f32[1,16,32,256]{3,2,1,0:T(8,128)S(1)} %get-tuple-element.25, f32[2,16,32,256]{3,2,1,0:T(8,128)S(1)} %copy-done, f32[3,16,32,1]{3,2,1,0:T(8,128)} %get-tuple-element.53, ...), kind=kLoop, calls=%fused_computation.94 | loop fusion | flops 655360 | bytes 5249024 | tf_op jit(solution)/shard_map/mul | solution.py:299
  76.4 2.0 %subtract_bitcast_fusion.2 = (f32[16,32,256]{2,1,0:T(8,128)}, f32[1,16,32,256]{3,2,1,0:T(8,128)}) fusion(f32[3,16,31,256]{3,2,1,0:T(8,128)S(1)} %copy-done.3, f32[3,16,1,256]{3,2,1,0:T(1,128)} %collective-permute-done.7), kind=kLoop, calls=%fused_computation.96 | loop fusion | flops 262144 | bytes 2621440 | tf_op jit(solution)/shard_map/mul | solution.py:299
  78.4 1.9 %subtract_bitcast_fusion.3 = (f32[16,32,256]{2,1,0:T(8,128)}, f32[1,16,32,256]{3,2,1,0:T(8,128)}) fusion(f32[3,16,1,256]{3,2,1,0:T(1,128)} %collective-permute-done.6, f32[3,16,31,256]{3,2,1,0:T(8,128)S(1)} %copy-done.1), kind=kLoop, calls=%fused_computation.97 | loop fusion | flops 262144 | bytes 2621440 | tf_op jit(solution)/shard_map/mul | solution.py:298
  84.1 3.7 %all-to-all-done.1 = f32[128,1,1224]{2,1,0:T(1,128)} async-done(((f32[128,1,1224]{2,1,0:T(1,128)}), f32[128,1,1224]{2,1,0:T(1,128)}, u32[]{:S(2)}, u32[]{:S(2)}) %all-to-all-start.1) | async-done | bytes 626720 | tf_op jit(solution)/shard_map/all_to_all | solution.py:140
  88.3 3.3 %reduce = f32[128,1224]{1,0:T(8,128)S(1)} reduce(f32[128,1,1224]{2,1,0:T(1,128)} %all-to-all-done.1, f32[]{:T(128)} %broadcast.284), dimensions={1}, to_apply=%all_to_all.7.reduce_sub_computation | reduce | bytes 1253380 | tf_op jit(solution)/shard_map/all_to_all | solution.py:140
  91.6 3.6 %reshape.211 = f32[128,18,2,34]{3,2,1,0:T(2,128)} reshape(f32[128,1224]{1,0:T(8,128)S(1)} %reduce) | data formatting | bytes 1253376
  95.3 3.0 %copy.286 = f32[128,2,18,34]{3,1,0,2:T(2,128)S(1)} copy(f32[128,2,18,34]{3,1,2,0:T(2,128)} %bitcast.676) | data formatting | bytes 1253376 | tf_op jit(solution)/shard_map/all_to_all | solution.py:140
  98.3 2.0 %convolution_multiply_fusion.1 = f32[18,34,256]{2,1,0:T(8,128)S(1)} fusion(f32[256,18,34]{2,0,1:T(8,128)S(1)} %bitcast.675, f32[256,256]{1,0:T(8,128)S(1)} %fusion.42), kind=kOutput, calls=%fused_computation.34 | convolution fusion | flops 240804864 | bytes 1515520 | tf_op jit(solution)/shard_map/nz,nxy->xyz/dot_general | solution.py:142
  101.8 15.3 %shard_map.67 = (f32[19,16,32,256]{3,2,1,0:T(8,128)}, f32[3,16,32,256]{3,2,1,0:T(8,128)S(1)}, f32[10,16,1,256]{3,2,1,0:T(1,128)S(1)}) custom-call(f32[19,16,32,256]{3,2,1,0:T(8,128)} %pop_ref.1, f32[16,32,256]{2,1,0:T(8,128)S(1)} %convert_element_type.50.fluid_ref, f32[3,16,32,256]{3,2,1,0:T(8,128)S(1)} %pad_maximum_fusion.push_ref), custom_call_target="tpu_custom_call" | custom-call | tf_op jit(solution)/shard_map/pallas_call | solution.py:229
  122.0 5.1 %collective-permute-start.1 = (f32[5,32,256]{2,1,0:T(8,128)S(1)}, f32[5,32,256]{2,1,0:T(8,128)S(1)}, u32[]{:S(2)}, u32[]{:S(2)}) collective-permute-start(f32[5,32,256]{2,1,0:T(8,128)S(1)} %get-tuple-element.27), channel_id=1, source_target_pairs={{0,112},{16,0},{32,16},{48,32},{64,48},{80,64},{96,80},{112,96},{1... | collective-permute-start | bytes 491528 | tf_op jit(solution)/shard_map/ppermute | solution.py:349
  127.4 4.9 %multiply_add_fusion = f32[2,16,32,256]{3,2,1,0:T(8,128)} fusion(f32[2,16,32,256]{3,2,1,0:T(8,128)S(1)} %copy-done, f32[1,16,32,256]{3,2,1,0:T(8,128)S(1)} %get-tuple-element.25, f32[3,16,32,1]{3,2,1,0:T(8,128)S(1)} %copy-done.14, f32[3,16,32,1]{3,2,1,0:T(8,128)S(1)} %copy-done.13, f32[3,16,32,255]{3,2,1,0:T(8,128)S(1)} %copy-done.6, ...), kind=kLoop, calls=%fused_computation.63 | loop fusion | flops 13893632 | bytes 20977672 | tf_op jit(solution)/shard_map/add | solution.py:306
  134.7 4.1 %collective-permute-done.2 = f32[5,16,1,256]{3,2,1,0:T(1,128)S(1)} collective-permute-done((f32[5,16,1,256]{3,2,1,0:T(1,128)S(1)}, f32[5,16,1,256]{3,2,1,0:T(1,128)S(1)}, u32[]{:S(2)}, u32[]{:S(2)}) %collective-permute-start.2) | collective-permute-done | bytes 81952 | tf_op jit(solution)/shard_map/ppermute | solution.py:364
  139.6 2.6 %shard_map.68 = f32[19,16,32,256]{3,2,1,0:T(8,128)} custom-call(f32[10,1,32,256]{3,2,1,0:T(8,128)} %copy-done.24, f32[10,16,1,256]{3,2,1,0:T(1,128)} %pad_maximum_fusion.14.cols_ref, f32[19,16,32,256]{3,2,1,0:T(8,128)} %get-tuple-element.12.wrapped_hbm), custom_call_target="tpu_custom_call", output_to_operand_aliasing={{}: (2, {})} | custom-call | tf_op jit(solution)/shard_map/pallas_call | solution.py:274
  (252 shorter events, 36.9 us)
Async XLA Ops:
  9.0 18.3 %copy-start.11 = (f32[16,32,256]{2,1,0:T(8,128)}, f32[16,32,256]{2,1,0:T(8,128)S(1)}, u32[]{:S(2)}) copy-start(f32[16,32,256]{2,1,0:T(8,128)S(1)} %fusion.39) | copy-start | bytes 1572868
  10.3 29.9 %all-to-all-start = ((f32[128,8,128]{2,1,0:T(8,128)}), f32[128,8,128]{2,1,0:T(8,128)}, u32[]{:S(2)}, u32[]{:S(2)}) async-start(f32[128,8,128]{2,1,0:T(8,128)} %reshape.198), calls=%async_computation | async-start | bytes 1048576 | tf_op jit(solution)/shard_map/all_to_all | solution.py:111
  22.7 53.7 %collective-permute-start.7 = (f32[3,16,1,256]{3,2,1,0:T(1,128)}, f32[3,16,1,256]{3,2,1,0:T(1,128)}, u32[]{:S(2)}, u32[]{:S(2)}) collective-permute-start(f32[3,16,1,256]{3,2,1,0:T(1,128)} %get-tuple-element.51), channel_id=1, source_target_pairs={{0,1},{1,2},{2,3},{3,4},{4,5},{5,6},{6,7},{7,8},{8,9},{9,10},{10,1... | collective-permute-start | bytes 147464 | tf_op jit(solution)/shard_map/ppermute | solution.py:57
  22.7 55.6 %collective-permute-start.6 = (f32[3,16,1,256]{3,2,1,0:T(1,128)}, f32[3,16,1,256]{3,2,1,0:T(1,128)}, u32[]{:S(2)}, u32[]{:S(2)}) collective-permute-start(f32[3,16,1,256]{3,2,1,0:T(1,128)} %get-tuple-element.50), channel_id=1, source_target_pairs={{0,15},{1,0},{2,1},{3,2},{4,3},{5,4},{6,5},{7,6},{8,7},{9,8},{10,9... | collective-permute-start | bytes 147464 | tf_op jit(solution)/shard_map/ppermute | solution.py:58
  27.3 53.0 %collective-permute-start.5 = (f32[3,1,32,256]{3,2,1,0:T(8,128)}, f32[3,1,32,256]{3,2,1,0:T(8,128)}, u32[]{:S(2)}, u32[]{:S(2)}) collective-permute-start(f32[3,1,32,256]{3,2,1,0:T(8,128)} %get-tuple-element.47), channel_id=1, source_target_pairs={{0,16},{16,32},{32,48},{48,64},{64,80},{80,96},{96,112},{112,0},{1... | collective-permute-start | bytes 294920 | tf_op jit(solution)/shard_map/ppermute | solution.py:57
  28.2 54.0 %collective-permute-start.4 = (f32[3,1,32,256]{3,2,1,0:T(8,128)}, f32[3,1,32,256]{3,2,1,0:T(8,128)}, u32[]{:S(2)}, u32[]{:S(2)}) collective-permute-start(f32[3,1,32,256]{3,2,1,0:T(8,128)} %get-tuple-element.46), channel_id=1, source_target_pairs={{0,112},{16,0},{32,16},{48,32},{64,48},{80,64},{96,80},{112,96},{1... | collective-permute-start | bytes 294920 | tf_op jit(solution)/shard_map/ppermute | solution.py:58
  35.0 38.5 %copy-start.5 = (f32[3,16,32,255]{3,2,1,0:T(8,128)}, f32[3,16,32,255]{3,2,1,0:T(8,128)S(1)}, u32[]{:S(2)}) copy-start(f32[3,16,32,255]{3,2,1,0:T(8,128)S(1)} %fusion.4) | copy-start | bytes 4700164
  67.5 20.3 %all-to-all-start.1 = ((f32[128,1,1224]{2,1,0:T(1,128)}), f32[128,1,1224]{2,1,0:T(1,128)}, u32[]{:S(2)}, u32[]{:S(2)}) async-start(f32[128,1,1224]{2,1,0:T(1,128)} %reshape.210), calls=%async_computation.1 | async-start | bytes 1310720 | tf_op jit(solution)/shard_map/all_to_all | solution.py:140
  101.7 25.6 %copy-start.6 = (f32[3,16,32,255]{3,2,1,0:T(8,128)S(1)}, f32[3,16,32,255]{3,2,1,0:T(8,128)}, u32[]{:S(2)}) copy-start(f32[3,16,32,255]{3,2,1,0:T(8,128)} %copy-done.5) | copy-start | bytes 4700164
  101.7 25.6 %copy-start.8 = (f32[3,15,32,256]{3,2,1,0:T(8,128)S(1)}, f32[3,15,32,256]{3,2,1,0:T(8,128)}, u32[]{:S(2)}) copy-start(f32[3,15,32,256]{3,2,1,0:T(8,128)} %get-tuple-element.44) | copy-start | bytes 4423684
  101.7 25.6 %copy-start.10 = (f32[3,15,32,256]{3,2,1,0:T(8,128)S(1)}, f32[3,15,32,256]{3,2,1,0:T(8,128)}, u32[]{:S(2)}) copy-start(f32[3,15,32,256]{3,2,1,0:T(8,128)} %get-tuple-element.45) | copy-start | bytes 4423684
  101.7 25.6 %copy-start.14 = (f32[3,16,32,1]{3,2,1,0:T(8,128)S(1)}, f32[3,16,32,1]{3,2,1,0:T(8,128)}, u32[]{:S(2)}) copy-start(f32[3,16,32,1]{3,2,1,0:T(8,128)} %get-tuple-element.53) | copy-start | bytes 18436
  101.7 25.6 %copy-start.17 = (f32[16,32,256]{2,1,0:T(8,128)S(1)}, f32[16,32,256]{2,1,0:T(8,128)}, u32[]{:S(2)}) copy-start(f32[16,32,256]{2,1,0:T(8,128)} %get-tuple-element.39) | copy-start | bytes 1572868
  101.7 25.6 %copy-start.18 = (f32[16,32,256]{2,1,0:T(8,128)S(1)}, f32[16,32,256]{2,1,0:T(8,128)}, u32[]{:S(2)}) copy-start(f32[16,32,256]{2,1,0:T(8,128)} %get-tuple-element.40) | copy-start | bytes 1572868
  101.8 25.6 %copy-start.19 = (f32[16,32,256]{2,1,0:T(8,128)S(1)}, f32[16,32,256]{2,1,0:T(8,128)}, u32[]{:S(2)}) copy-start(f32[16,32,256]{2,1,0:T(8,128)} %get-tuple-element.37) | copy-start | bytes 1572868
  101.8 25.6 %copy-start.20 = (f32[16,32,256]{2,1,0:T(8,128)S(1)}, f32[16,32,256]{2,1,0:T(8,128)}, u32[]{:S(2)}) copy-start(f32[16,32,256]{2,1,0:T(8,128)} %get-tuple-element.38) | copy-start | bytes 1572868
  101.8 25.6 %copy-start.21 = (f32[16,32,256]{2,1,0:T(8,128)S(1)}, f32[16,32,256]{2,1,0:T(8,128)}, u32[]{:S(2)}) copy-start(f32[16,32,256]{2,1,0:T(8,128)} %get-tuple-element.17) | copy-start | bytes 1572868
  117.1 10.3 %copy-start.4 = (f32[3,16,31,256]{3,2,1,0:T(8,128)S(1)}, f32[3,16,31,256]{3,2,1,0:T(8,128)}, u32[]{:S(2)}) copy-start(f32[3,16,31,256]{3,2,1,0:T(8,128)} %get-tuple-element.49) | copy-start | bytes 4571140
  117.1 10.3 %copy-start.13 = (f32[3,16,32,1]{3,2,1,0:T(8,128)S(1)}, f32[3,16,32,1]{3,2,1,0:T(8,128)}, u32[]{:S(2)}) copy-start(f32[3,16,32,1]{3,2,1,0:T(8,128)} %get-tuple-element.52) | copy-start | bytes 18436
  117.1 10.3 %copy-start.25 = (f32[2]{0:T(128)S(1)}, f32[2]{0:T(128)}, u32[]{:S(2)}) copy-start(f32[2]{0:T(128)} %constant.105.clone) | copy-start | bytes 28
  121.4 10.9 %collective-permute-start = (f32[5,32,256]{2,1,0:T(8,128)S(1)}, f32[5,32,256]{2,1,0:T(8,128)S(1)}, u32[]{:S(2)}, u32[]{:S(2)}) collective-permute-start(f32[5,32,256]{2,1,0:T(8,128)S(1)} %get-tuple-element.28), channel_id=1, source_target_pairs={{0,16},{16,32},{32,48},{48,64},{64,80},{80,96},{96,112},{112,0},{1... | collective-permute-start | bytes 491528 | tf_op jit(solution)/shard_map/ppermute | solution.py:349
  122.0 10.4 %collective-permute-start.1 = (f32[5,32,256]{2,1,0:T(8,128)S(1)}, f32[5,32,256]{2,1,0:T(8,128)S(1)}, u32[]{:S(2)}, u32[]{:S(2)}) collective-permute-start(f32[5,32,256]{2,1,0:T(8,128)S(1)} %get-tuple-element.27), channel_id=1, source_target_pairs={{0,112},{16,0},{32,16},{48,32},{64,48},{80,64},{96,80},{112,96},{1... | collective-permute-start | bytes 491528 | tf_op jit(solution)/shard_map/ppermute | solution.py:349
  132.5 2.1 %collective-permute-start.3 = (f32[5,16,1,256]{3,2,1,0:T(1,128)S(1)}, f32[5,16,1,256]{3,2,1,0:T(1,128)S(1)}, u32[]{:S(2)}, u32[]{:S(2)}) collective-permute-start(f32[5,16,1,256]{3,2,1,0:T(1,128)S(1)} %pad_maximum_fusion.17), channel_id=1, source_target_pairs={{0,15},{1,0},{2,1},{3,2},{4,3},{5,4},{6,5},{7,6},{8,7},{9,8},{10,9... | collective-permute-start | bytes 245768 | tf_op jit(solution)/shard_map/ppermute | solution.py:364
  132.8 6.0 %collective-permute-start.2 = (f32[5,16,1,256]{3,2,1,0:T(1,128)S(1)}, f32[5,16,1,256]{3,2,1,0:T(1,128)S(1)}, u32[]{:S(2)}, u32[]{:S(2)}) collective-permute-start(f32[5,16,1,256]{3,2,1,0:T(1,128)S(1)} %pad_maximum_fusion.16), channel_id=1, source_target_pairs={{0,1},{1,2},{2,3},{3,4},{4,5},{5,6},{6,7},{7,8},{8,9},{9,10},{10,1... | collective-permute-start | bytes 245768 | tf_op jit(solution)/shard_map/ppermute | solution.py:364
  (12 other events, 53.6 us)
